TPU v7x, 512 devices: a whole 4x8x8 slice. The times are simulated.
512 devices in a mesh: seq: 64 (over x, z_lo, y), tp: 8 (over z_hi, core).
Axes of the slice: x: 4, y: 8, z: 8 (z_hi: 4, z_lo: 2; z = z_hi * 2 + z_lo), core: 2. Of those that a mesh axis runs over, the one named last changes fastest.
Arguments:
- tokens: bfloat16 [16384, 2048], P('seq', 'tp'), may hold values from -6 to 6
- key_weight: bfloat16 [2048, 2048], P(None, 'tp'), may hold values from -0.125 to 0.125
- value_weight: bfloat16 [2048, 2048], P(None, 'tp'), may hold values from -0.125 to 0.125
- queries: bfloat16 [16384, 2, 2048], P('seq', None, 'tp'), may hold values from -256 to 256
- prompt_pages: int32 [16], replicated, may hold values from 1 to 97, 1024 in all
- page_table: int32 [1024], P('seq'), may hold values from 0 to 1023, as said below
Outputs:
- attended: bfloat16 [16384, 2, 2048], P('seq', None, 'tp')
- cache: bfloat16 [1024, 16, 2, 2048], P('seq', None, None, 'tp')
Inputs may be any that keep to these rules, and one draw needn't show every extreme that they name: `prompt_pages`: lengths of the prompts in pages; they sum to 1024 and the longest has exactly 97 pages. `page_table`: A permutation of the cache pages. Page c is held by owner c // 16 of seq. At most 1 pages of one stream block go to one owner, some block sends exactly 1 to one owner, and every owner receives 256/16 pages.
All inputs are finite; a program needn't handle non-finite values.
Results may differ from a plain program's by a relative error of at most 0.03.
Values may be sent and summed in bfloat16 or wider, within the bound.
No kernel may reach another device: no remote copies, remote signals or barrier semaphores. Data moves between devices by JAX's collectives and lax.ppermute only.
A program may use at most 64 MiB of HBM per device.

v0:
```python
import functools
import math

import jax
import jax.numpy as jnp
from jax import lax
from jax.experimental import pallas as pl
from jax.sharding import PartitionSpec as P


HD = 128
TOPK = 2
PAGE = 16
BACK = 6


def from_behind(value, axis, by):
    peers = lax.axis_size(axis)
    pairs = [(i, i + by) for i in range(peers) if 0 <= i + by < peers]
    return lax.ppermute(value, axis, pairs)


def segment_info(positions, prompt_pages):
    ends = PAGE * jnp.cumsum(prompt_pages)
    below = ends[None, :] <= positions[:, None]
    segment = jnp.sum(below.astype(jnp.int32), axis=1)
    start = jnp.max(jnp.where(below, ends[None, :], 0), axis=1)
    return (segment, positions - start)


def rotate_heads(raw, offsets):
    half = HD // 2
    inverse = 10000.0 ** (-(2.0 * jnp.arange(half, dtype=jnp.float32)) / HD)
    angle = offsets.astype(jnp.float32)[:, None] * inverse[None, :]
    cosine = jnp.cos(angle)[:, None, :]
    sine = jnp.sin(angle)[:, None, :]
    lower = raw[..., :half]
    upper = raw[..., half:]
    return jnp.concatenate([lower * cosine - upper * sine, upper * cosine + lower * sine], axis=-1)


def attention_kernel(query_segment_ref, key_segment_ref, query_ref, *refs, blocks, scale):
    key_refs = refs[:blocks]
    value_refs = refs[blocks : 2 * blocks]
    out_ref = refs[2 * blocks]
    rows = query_ref.shape[0]
    query = query_ref[...]
    query_segment = query_segment_ref[...]
    row = lax.broadcasted_iota(jnp.int32, (rows, rows), 0)
    col = lax.broadcasted_iota(jnp.int32, (rows, rows), 1)

    def scores(distance):
        key = key_refs[distance][...]
        product = lax.dot_general(
            query, key, (((1,), (1,)), ((), ())), preferred_element_type=jnp.float32
        )
        allowed = query_segment == key_segment_ref[pl.ds(distance, 1), :]
        if distance == 0:
            allowed = allowed & (col <= row)
        return jnp.where(allowed, product * scale, -jnp.inf)

    peak = jnp.max(scores(0), axis=1, keepdims=True)
    for distance in range(1, blocks):
        peak = jnp.maximum(peak, jnp.max(scores(distance), axis=1, keepdims=True))
    total = jnp.zeros((rows, 1), jnp.float32)
    summed = jnp.zeros((rows, out_ref.shape[1]), jnp.float32)
    for distance in range(blocks):
        weight = jnp.exp(scores(distance) - peak)
        total = total + jnp.sum(weight, axis=1, keepdims=True)
        summed = summed + jnp.dot(
            weight.astype(jnp.bfloat16),
            value_refs[distance][...],
            preferred_element_type=jnp.float32,
        )
    out_ref[...] = (summed / total).astype(out_ref.dtype)


def attend(query, query_segment, key_segment, sources, local_heads):
    rows = query.shape[0]
    blocks = len(sources)
    grid = (local_heads, TOPK)
    query_spec = pl.BlockSpec((rows, HD), lambda h, e: (0, e * local_heads + h))

    def column_spec(base):
        return pl.BlockSpec((rows, HD), lambda h, e: (0, base + h))

    key_specs = [column_spec(base) for _, base in sources]
    value_specs = [column_spec(base + local_heads) for _, base in sources]
    in_specs = (
        [
            pl.BlockSpec((rows, 1), lambda h, e: (0, 0)),
            pl.BlockSpec((blocks, rows), lambda h, e: (0, 0)),
            query_spec,
        ]
        + key_specs
        + value_specs
    )
    arrays = [array for array, _ in sources]
    combos = local_heads * TOPK
    cost = pl.CostEstimate(
        flops=combos * 3 * blocks * 2 * rows * rows * HD,
        transcendentals=combos * blocks * rows * rows,
        bytes_accessed=2 * query.size * 2 + blocks * rows * 2 * local_heads * HD * 2,
    )
    kernel = functools.partial(attention_kernel, blocks=blocks, scale=1.0 / math.sqrt(HD))
    return pl.pallas_call(
        kernel,
        grid=grid,
        in_specs=in_specs,
        out_specs=query_spec,
        out_shape=jax.ShapeDtypeStruct(query.shape, jnp.bfloat16),
        cost_estimate=cost,
        name="block_attention",
    )(query_segment, key_segment, query, *arrays, *arrays)


def body(tokens, key_weight, value_weight, queries, prompt_pages, page_table):
    block_rows = tokens.shape[0]
    width = key_weight.shape[1]
    local_heads = width // HD
    devices = lax.axis_size("seq")
    first_row = lax.axis_index("seq") * block_rows
    positions = first_row + jnp.arange(block_rows, dtype=jnp.int32)
    segment, offsets = segment_info(positions, prompt_pages)
    piece = lax.all_gather(tokens, "tp", axis=1, tiled=True)
    raw_keys = jnp.dot(piece, key_weight, preferred_element_type=jnp.float32)
    raw_values = jnp.dot(piece, value_weight, preferred_element_type=jnp.float32)
    keys = rotate_heads(raw_keys.reshape(block_rows, local_heads, HD), offsets).astype(jnp.bfloat16)
    values = raw_values.astype(jnp.bfloat16)
    key_value = jnp.concatenate([keys.reshape(block_rows, width), values], axis=1)
    odd = [from_behind(key_value, "seq", distance) for distance in range(1, BACK + 1, 2)]
    even = from_behind(jnp.concatenate(odd, axis=1), "seq", 1)
    span = 2 * local_heads
    sources = [(key_value, 0)]
    for distance in range(1, BACK + 1):
        if distance % 2:
            sources.append((odd[distance // 2], 0))
        else:
            sources.append((even, span * (distance // 2 - 1)))
    key_place = positions[None, :] - block_rows * jnp.arange(BACK + 1, dtype=jnp.int32)[:, None]
    key_segment, _ = segment_info(key_place.reshape(-1), prompt_pages)
    key_segment = jnp.where(key_place >= 0, key_segment.reshape(BACK + 1, block_rows), -1)
    query = queries.reshape(block_rows, TOPK * width)
    attended = attend(query, segment[:, None], key_segment, sources, local_heads)
    attended = attended.reshape(block_rows, TOPK, width)
    pages_dev = block_rows // PAGE
    capacity = max(1, pages_dev // devices)
    owner = page_table // pages_dev
    place_on_owner = page_table % pages_dev
    page_order = jnp.arange(pages_dev, dtype=jnp.int32)
    earlier = (owner[:, None] == owner[None, :]) & (page_order[None, :] < page_order[:, None])
    rank = jnp.sum(earlier.astype(jnp.int32), axis=1)
    target = (owner[None, None, :] == jnp.arange(devices, dtype=jnp.int32)[:, None, None]) & (
        rank[None, None, :] == jnp.arange(capacity, dtype=jnp.int32)[None, :, None]
    )
    pages = key_value.reshape(pages_dev, PAGE, 2, width)
    page_index = jnp.sum(jnp.where(target, page_order[None, None, :], 0), axis=2)
    outgoing = pages[page_index.reshape(-1)]
    labels = jnp.sum(jnp.where(target, place_on_owner[None, None, :] + 1, 0), axis=2) - 1
    incoming = lax.all_to_all(outgoing, "seq", split_axis=0, concat_axis=0, tiled=True)
    arrived = lax.all_to_all(labels, "seq", split_axis=0, concat_axis=0, tiled=True)
    slots = jnp.arange(devices * capacity, dtype=jnp.int32)
    source_slot = jnp.sum(
        jnp.where(arrived.reshape(-1)[None, :] == page_order[:, None], slots[None, :], 0), axis=1
    )
    cache = incoming[source_slot]
    return (attended, cache)


def solution(mesh):
    in_specs = (P("seq", "tp"), P(None, "tp"), P(None, "tp"), P("seq", None, "tp"), P(), P("seq"))
    out_specs = (P("seq", None, "tp"), P("seq", None, None, "tp"))
    return jax.shard_map(body, mesh=mesh, in_specs=in_specs, out_specs=out_specs, check_vma=False)
```

profile of v0, /device:TPU:6, one launch (start us, length us, event | category | flops | bytes accessed | tf_op | source)
XLA Modules:
  0.0 158.7 jit_solution(3802686527182407135)
XLA Ops:
  7.2 0.0 copy-start
  7.2 0.0 all-gather.2.cloned.1.call-start
  7.2 0.7 all-gather.2.cloned.1.call-update
  7.9 0.7 and_select_fusion.1
  8.6 0.2 convert_reduce_fusion.1
  8.8 0.1 select_reduce_fusion.1
  8.9 0.7 copy.47
  9.6 12.8 %all-to-all-start.1 = ((s32[64,1,1]{2,1,0:T(1,128)}), s32[64,1,1]{2,1,0:T(1,128)}, u32[]{:S(2)}, u32[]{:S(2)}) async-start(s32[64,1,1]{2,1,0:T(1,128)} %copy.47), calls=%async_computation.1 | async-start | bytes 65536 | tf_op jit(solution)/shard_map/all_to_all | solution.py:161
  22.4 0.7 copy.41
  23.2 0.1 multiply_reduce_fusion
  23.3 0.1 fusion.1
  23.4 1.2 multiply_cosine_fusion
  24.6 24.6 %all-gather.2.cloned.1.call-done = bf16[256,2048]{1,0:T(8,128)(2,1)} async-done(((bf16[256,256]{1,0:T(8,128)(2,1)}), bf16[256,2048]{1,0:T(8,128)(2,1)}) %all-gather.2.cloned.1.call-update) | async-done | bytes 1048592 | tf_op jit(solution)/shard_map/all_gather | solution.py:125
  49.2 1.7 %fusion.8 = f32[256,256]{0,1:T(8,128)S(1)} fusion(bf16[256,2048]{1,0:T(8,128)(2,1)} %all-gather.2.cloned.1.call-done, bf16[2048,256]{1,0:T(8,128)(2,1)S(1)} %copy-done), kind=kOutput, calls=%fused_computation.47 | convolution fusion | flops 268435456 | bytes 2359296 | tf_op jit(solution)/shard_map/dot_general | solution.py:126
  51.0 0.1 copy.50
  51.2 0.0 copy-start.7
  51.2 0.8 copy.51
  52.0 1.3 subtract_convert_fusion
  53.4 0.4 pad_maximum_fusion.2
  53.8 0.4 convolution_convert_fusion
  54.2 0.0 copy-start.2
  54.3 0.1 reshape.321
  54.4 1.6 %gather_fusion = bf16[64,16,2,256]{3,1,2,0:T(8,128)(2,1)} fusion(bf16[16,16,2,256]{3,1,2,0:T(8,128)(2,1)S(1)} %copy.46, s32[1024]{0:T(1024)S(1)} %pad_clamp_fusion.1), kind=kCustom, calls=%fused_computation | custom fusion | bytes 2097408 | tf_op jit(solution)/shard_map/gather | solution.py:158
  56.0 0.0 all-to-all-done.1
  56.0 10.6 %all-to-all-start = ((bf16[64,16,2,256]{3,1,2,0:T(8,128)(2,1)}), bf16[64,16,2,256]{3,1,2,0:T(8,128)(2,1)}, u32[]{:S(2)}, u32[]{:S(2)}) async-start(bf16[64,16,2,256]{3,1,2,0:T(8,128)(2,1)} %gather_fusion), calls=%async_computation | async-start | bytes 2097152 | tf_op jit(solution)/shard_map/all_to_all | solution.py:160
  66.6 0.0 copy-start.8
  66.6 3.5 %collective-permute-start = (bf16[256,512]{1,0:T(8,128)(2,1)S(1)}, bf16[256,512]{1,0:T(8,128)(2,1)S(1)}, u32[]{:S(2)}, u32[]{:S(2)}) collective-permute-start(bf16[256,512]{1,0:T(8,128)(2,1)S(1)} %pad_maximum_fusion.1.refs_0_.refs_7_), channel_id=1, source_target_pairs={{0,8},{8,16},{16,24},{24,32},{32,40},{40,48},{48,56},{56,64},{64,7... | collective-permute-start | bytes 786440 | tf_op jit(solution)/shard_map/ppermute | solution.py:20
  70.1 6.4 %collective-permute-start.1 = (bf16[256,512]{1,0:T(8,128)(2,1)S(1)}, bf16[256,512]{1,0:T(8,128)(2,1)S(1)}, u32[]{:S(2)}, u32[]{:S(2)}) collective-permute-start(bf16[256,512]{1,0:T(8,128)(2,1)S(1)} %pad_maximum_fusion.1.refs_0_.refs_7_), channel_id=1, source_target_pairs={{0,24},{8,32},{16,40},{24,48},{32,56},{40,64},{48,72},{56,80},{64,... | collective-permute-start | bytes 786440 | tf_op jit(solution)/shard_map/ppermute | solution.py:20
  76.5 3.4 %collective-permute-start.2 = (bf16[256,512]{1,0:T(8,128)(2,1)S(1)}, bf16[256,512]{1,0:T(8,128)(2,1)S(1)}, u32[]{:S(2)}, u32[]{:S(2)}) collective-permute-start(bf16[256,512]{1,0:T(8,128)(2,1)S(1)} %pad_maximum_fusion.1.refs_0_.refs_7_), channel_id=1, source_target_pairs={{0,40},{8,48},{16,56},{24,64},{32,72},{40,80},{48,88},{56,96},{64,... | collective-permute-start | bytes 786440 | tf_op jit(solution)/shard_map/ppermute | solution.py:20
  79.9 0.1 broadcast_subtract_fusion
  80.0 24.3 %collective-permute-done.refs_1_.refs_8_ = bf16[256,512]{1,0:T(8,128)(2,1)S(1)} collective-permute-done((bf16[256,512]{1,0:T(8,128)(2,1)S(1)}, bf16[256,512]{1,0:T(8,128)(2,1)S(1)}, u32[]{:S(2)}, u32[]{:S(2)}) %collective-permute-start) | collective-permute-done | bytes 262176 | tf_op jit(solution)/shard_map/ppermute | solution.py:20
  104.3 12.2 %collective-permute-done.1.refs_3_.refs_10_ = bf16[256,512]{1,0:T(8,128)(2,1)S(1)} collective-permute-done((bf16[256,512]{1,0:T(8,128)(2,1)S(1)}, bf16[256,512]{1,0:T(8,128)(2,1)S(1)}, u32[]{:S(2)}, u32[]{:S(2)}) %collective-permute-start.1) | collective-permute-done | bytes 262176 | tf_op jit(solution)/shard_map/ppermute | solution.py:20
  116.5 0.0 collective-permute-done.2.refs_5_.refs_12_
  116.5 1.0 pad_maximum_fusion
  117.5 2.2 %collective-permute-start.3 = (bf16[256,1536]{1,0:T(8,128)(2,1)}, bf16[256,1536]{1,0:T(8,128)(2,1)S(1)}, u32[]{:S(2)}, u32[]{:S(2)}) collective-permute-start(bf16[256,1536]{1,0:T(8,128)(2,1)} %pad_maximum_fusion), channel_id=1, source_target_pairs={{0,8},{8,16},{16,24},{24,32},{32,40},{40,48},{48,56},{56,64},{64,7... | collective-permute-start | bytes 2359304 | tf_op jit(solution)/shard_map/ppermute | solution.py:20
  119.7 0.1 convert_reduce_fusion
  119.8 0.8 copy.45.query_segment_ref
  120.6 0.7 copy.52
  121.4 0.7 compare_select_fusion.1.key_segment_ref
  122.0 2.0 %reduce.3 = s32[64]{0:T(128)S(1)} reduce(s32[64,1,1]{2,1,0:T(1,128)} %all-to-all-done.1, s32[]{:T(128)} %constant.26.clone.1), dimensions={1,2}, to_apply=%all_to_all.8.reduce_sub_computation | reduce | bytes 516 | tf_op jit(solution)/shard_map/all_to_all | solution.py:161
  124.0 0.1 select_reduce_fusion
  124.2 16.0 %collective-permute-done.3.refs_2_.refs_4_.refs_6_.refs_9_.refs_11_.refs_13_ = bf16[256,1536]{1,0:T(8,128)(2,1)S(1)} collective-permute-done((bf16[256,1536]{1,0:T(8,128)(2,1)}, bf16[256,1536]{1,0:T(8,128)(2,1)S(1)}, u32[]{:S(2)}, u32[]{:S(2)}) %collective-permute-start.3) | collective-permute-done | bytes 786464 | tf_op jit(solution)/shard_map/ppermute | solution.py:20
  140.1 0.9 copy-done.1
  141.0 6.3 %block_attention.1 = bf16[256,512]{1,0:T(8,128)(2,1)} custom-call(s32[256,1]{1,0:T(8,128)} %copy.45.query_segment_ref, s32[7,256]{1,0:T(8,128)} %compare_select_fusion.1.key_segment_ref, bf16[256,512]{1,0:T(8,128)(2,1)} %bitcast.23, bf16[256,512]{1,0:T(8,128)(2,1)} %copy-done.2, bf16[256,512]{1,0:T(8,128)(2,1)} %copy-done.4, bf16[256,1536]{1,0:T(8,128)(2,1)} %copy-done.1, ...), custom_call_target="tpu_custom_call" | custom-call | flops 1409286144 | bytes 2359296 | tf_op jit(solution)/shard_map/block_attention/pallas_call | solution.py:106
  147.4 1.7 %reshape.320 = bf16[256,2,256]{2,1,0:T(2,128)(2,1)} reshape(bf16[256,512]{1,0:T(8,128)(2,1)} %block_attention.1) | data formatting | bytes 524288 | tf_op jit(solution)/shard_map/reshape | solution.py:145
  149.1 0.0 all-to-all-done
  149.1 1.8 %gather_fusion.1 = bf16[16,16,2,256]{3,1,2,0:T(8,128)(2,1)S(1)} fusion(bf16[64,16,2,256]{3,1,2,0:T(8,128)(2,1)} %all-to-all-done, s32[1024]{0:T(1024)S(1)} %pad_clamp_fusion), kind=kCustom, calls=%fused_computation.1 | custom fusion | bytes 524352 | tf_op jit(solution)/shard_map/gather | solution.py:166
  150.9 0.9 copy.48
  (30 shorter events, 0.2 us)
Async XLA Ops:
  7.2 42.1 %copy-start = (bf16[2048,256]{1,0:T(8,128)(2,1)S(1)}, bf16[2048,256]{1,0:T(8,128)(2,1)}, u32[]{:S(2)}) copy-start(bf16[2048,256]{1,0:T(8,128)(2,1)} %param.7) | copy-start | bytes 3145732
  7.2 42.0 %all-gather.2.cloned.1.call-start = ((), (), s32[]{:S(2)}) async-start(), calls=%async_computation.2 | async-start | bytes 1179648 | tf_op jit(solution)/shard_map/all_gather | solution.py:125
  9.6 46.4 %all-to-all-start.1 = ((s32[64,1,1]{2,1,0:T(1,128)}), s32[64,1,1]{2,1,0:T(1,128)}, u32[]{:S(2)}, u32[]{:S(2)}) async-start(s32[64,1,1]{2,1,0:T(1,128)} %copy.47), calls=%async_computation.1 | async-start | bytes 65536 | tf_op jit(solution)/shard_map/all_to_all | solution.py:161
  51.2 2.6 %copy-start.3 = (bf16[256,2048]{1,0:T(8,128)(2,1)S(1)}, bf16[256,2048]{1,0:T(8,128)(2,1)}, u32[]{:S(2)}) copy-start(bf16[256,2048]{1,0:T(8,128)(2,1)} %all-gather.2.cloned.1.call-done) | copy-start | bytes 3145732
  51.2 2.6 %copy-start.7 = (bf16[2048,256]{1,0:T(8,128)(2,1)S(1)}, bf16[2048,256]{1,0:T(8,128)(2,1)}, u32[]{:S(2)}) copy-start(bf16[2048,256]{1,0:T(8,128)(2,1)} %param.8) | copy-start | bytes 3145732
  54.2 22.3 %copy-start.2 = (bf16[256,512]{1,0:T(8,128)(2,1)}, bf16[256,512]{1,0:T(8,128)(2,1)S(1)}, u32[]{:S(2)}) copy-start(bf16[256,512]{1,0:T(8,128)(2,1)S(1)} %pad_maximum_fusion.1.refs_0_.refs_7_) | copy-start | bytes 786436
  56.0 93.1 %all-to-all-start = ((bf16[64,16,2,256]{3,1,2,0:T(8,128)(2,1)}), bf16[64,16,2,256]{3,1,2,0:T(8,128)(2,1)}, u32[]{:S(2)}, u32[]{:S(2)}) async-start(bf16[64,16,2,256]{3,1,2,0:T(8,128)(2,1)} %gather_fusion), calls=%async_computation | async-start | bytes 2097152 | tf_op jit(solution)/shard_map/all_to_all | solution.py:160
  66.6 54.1 %copy-start.8 = (bf16[256,2,256]{2,1,0:T(2,128)(2,1)S(1)}, bf16[256,2,256]{2,1,0:T(2,128)(2,1)}, u32[]{:S(2)}) copy-start(bf16[256,2,256]{2,1,0:T(2,128)(2,1)} %param.9) | copy-start | bytes 786436
  66.6 37.7 %collective-permute-start = (bf16[256,512]{1,0:T(8,128)(2,1)S(1)}, bf16[256,512]{1,0:T(8,128)(2,1)S(1)}, u32[]{:S(2)}, u32[]{:S(2)}) collective-permute-start(bf16[256,512]{1,0:T(8,128)(2,1)S(1)} %pad_maximum_fusion.1.refs_0_.refs_7_), channel_id=1, source_target_pairs={{0,8},{8,16},{16,24},{24,32},{32,40},{40,48},{48,56},{56,64},{64,7... | collective-permute-start | bytes 786440 | tf_op jit(solution)/shard_map/ppermute | solution.py:20
  70.1 46.4 %collective-permute-start.1 = (bf16[256,512]{1,0:T(8,128)(2,1)S(1)}, bf16[256,512]{1,0:T(8,128)(2,1)S(1)}, u32[]{:S(2)}, u32[]{:S(2)}) collective-permute-start(bf16[256,512]{1,0:T(8,128)(2,1)S(1)} %pad_maximum_fusion.1.refs_0_.refs_7_), channel_id=1, source_target_pairs={{0,24},{8,32},{16,40},{24,48},{32,56},{40,64},{48,72},{56,80},{64,... | collective-permute-start | bytes 786440 | tf_op jit(solution)/shard_map/ppermute | solution.py:20
  76.5 40.0 %collective-permute-start.2 = (bf16[256,512]{1,0:T(8,128)(2,1)S(1)}, bf16[256,512]{1,0:T(8,128)(2,1)S(1)}, u32[]{:S(2)}, u32[]{:S(2)}) collective-permute-start(bf16[256,512]{1,0:T(8,128)(2,1)S(1)} %pad_maximum_fusion.1.refs_0_.refs_7_), channel_id=1, source_target_pairs={{0,40},{8,48},{16,56},{24,64},{32,72},{40,80},{48,88},{56,96},{64,... | collective-permute-start | bytes 786440 | tf_op jit(solution)/shard_map/ppermute | solution.py:20
  104.3 17.1 %copy-start.4 = (bf16[256,512]{1,0:T(8,128)(2,1)}, bf16[256,512]{1,0:T(8,128)(2,1)S(1)}, u32[]{:S(2)}) copy-start(bf16[256,512]{1,0:T(8,128)(2,1)S(1)} %collective-permute-done.refs_1_.refs_8_) | copy-start | bytes 786436
  116.5 4.9 %copy-start.5 = (bf16[256,512]{1,0:T(8,128)(2,1)}, bf16[256,512]{1,0:T(8,128)(2,1)S(1)}, u32[]{:S(2)}) copy-start(bf16[256,512]{1,0:T(8,128)(2,1)S(1)} %collective-permute-done.1.refs_3_.refs_10_) | copy-start | bytes 786436
  116.5 4.9 %copy-start.6 = (bf16[256,512]{1,0:T(8,128)(2,1)}, bf16[256,512]{1,0:T(8,128)(2,1)S(1)}, u32[]{:S(2)}) copy-start(bf16[256,512]{1,0:T(8,128)(2,1)S(1)} %collective-permute-done.2.refs_5_.refs_12_) | copy-start | bytes 786436
  117.5 22.6 %collective-permute-start.3 = (bf16[256,1536]{1,0:T(8,128)(2,1)}, bf16[256,1536]{1,0:T(8,128)(2,1)S(1)}, u32[]{:S(2)}, u32[]{:S(2)}) collective-permute-start(bf16[256,1536]{1,0:T(8,128)(2,1)} %pad_maximum_fusion), channel_id=1, source_target_pairs={{0,8},{8,16},{16,24},{24,32},{32,40},{40,48},{48,56},{56,64},{64,7... | collective-permute-start | bytes 2359304 | tf_op jit(solution)/shard_map/ppermute | solution.py:20
  140.1 0.9 copy-start.1
Sparse Core Ops, SparseCore 0:
  10.1 39.0 all-gather.1
where the time goes:
time: 159 us
  waiting for transfers between devices  77.7 us (49%)
  starting transfers between devices  39 us (25%)
  between operations  14.3 us (9%)
  local copies, waits for them, and re-layouts  11.1 us (7%)
  other arithmetic  8.11 us (5%)
  Pallas kernels  6.34 us (4%)
  matrix products  2.19 us (1%)
    ppermute x4, waiting for transfers between devices, from_behind(): return lax.ppermute(value, axis, pairs)  52.4 us
    all_gather x1, waiting for transfers between devices, body(): piece = lax.all_gather(tokens, 'tp', axis=1, tiled=True)  24.6 us
    ppermute x4, starting transfers between devices, from_behind(): return lax.ppermute(value, axis, pairs)  15.5 us
    all_to_all x1, starting transfers between devices, body(): lax.all_to_all(labels, 'seq', split_axis=0, concat_axis=0, tiled=True)  12.8 us
    all_to_all x1, starting transfers between devices, body(): lax.all_to_all(outgoing, 'seq', split_axis=0, concat_axis=0, tiled=True)  10.6 us
    pallas_call x1, Pallas kernels, attend(): pl.pallas_call(kernel, grid=grid, in_specs=in_specs, out_specs=query_spec...  6.34 us
    unnamed x23, local copies, waits for them, and re-layouts  3.63 us
  transfers between devices with their start and end apart: 7, of which 4 were waited for; matrix products, arithmetic and copies ran while one was open for 11% of the time, Pallas kernels for 4%

commit v1 on v0

--- a/solution.py
+++ b/solution.py
@@ -128,15 +128,19 @@
     keys = rotate_heads(raw_keys.reshape(block_rows, local_heads, HD), offsets).astype(jnp.bfloat16)
     values = raw_values.astype(jnp.bfloat16)
     key_value = jnp.concatenate([keys.reshape(block_rows, width), values], axis=1)
-    odd = [from_behind(key_value, "seq", distance) for distance in range(1, BACK + 1, 2)]
-    even = from_behind(jnp.concatenate(odd, axis=1), "seq", 1)
+    direct = (1, 3, 5, 6)
+    sent = {distance: from_behind(key_value, "seq", distance) for distance in direct}
+    relayed = [distance for distance in range(2, BACK + 1) if distance not in direct]
+    onward = from_behind(
+        jnp.concatenate([sent[distance - 1] for distance in relayed], axis=1), "seq", 1
+    )
     span = 2 * local_heads
     sources = [(key_value, 0)]
     for distance in range(1, BACK + 1):
-        if distance % 2:
-            sources.append((odd[distance // 2], 0))
+        if distance in sent:
+            sources.append((sent[distance], 0))
         else:
-            sources.append((even, span * (distance // 2 - 1)))
+            sources.append((onward, span * relayed.index(distance)))
     key_place = positions[None, :] - block_rows * jnp.arange(BACK + 1, dtype=jnp.int32)[:, None]
     key_segment, _ = segment_info(key_place.reshape(-1), prompt_pages)
     key_segment = jnp.where(key_place >= 0, key_segment.reshape(BACK + 1, block_rows), -1)

time: 159 us -> 178 us (1.12)
  waiting for transfers between devices: 77.7 us -> 94.4 us
  starting transfers between devices: 39 us -> 41.9 us
    ppermute x4 -> x5, waiting for transfers between devices: 52.4 us -> 68.5 us  [from_behind(): return lax.ppermute(value, axis, pairs)]
    ppermute x4 -> x5, starting transfers between devices: 15.5 us -> 18.6 us  [from_behind(): return lax.ppermute(value, axis, pairs)]
    unnamed x23 -> x27, local copies, waits for them, and re-layouts: 3.63 us -> 5.21 us
  transfers between devices with their start and end apart: 7 -> 8, of which waited for: 4 -> 5; matrix products, arithmetic and copies ran while one was open for 11% -> 10% of each run, Pallas kernels for 4% -> 4%
where the time goes in v1:
time: 178 us; the launch traced here: 177 us
  waiting for transfers between devices  94.4 us (53%)
  starting transfers between devices  41.9 us (24%)
  between operations  14.3 us (8%)
  local copies, waits for them, and re-layouts  10.8 us (6%)
  other arithmetic  7.36 us (4%)
  Pallas kernels  6.28 us (4%)
  matrix products  2.19 us (1%)
    ppermute x5, waiting for transfers between devices, from_behind(): return lax.ppermute(value, axis, pairs)  68.5 us
    all_gather x1, waiting for transfers between devices, body(): piece = lax.all_gather(tokens, 'tp', axis=1, tiled=True)  25.2 us
    ppermute x5, starting transfers between devices, from_behind(): return lax.ppermute(value, axis, pairs)  18.6 us
    all_to_all x1, starting transfers between devices, body(): lax.all_to_all(labels, 'seq', split_axis=0, concat_axis=0, tiled=True)  12.8 us
    all_to_all x1, starting transfers between devices, body(): lax.all_to_all(outgoing, 'seq', split_axis=0, concat_axis=0, tiled=True)  10.4 us
    pallas_call x1, Pallas kernels, attend(): pl.pallas_call(kernel, grid=grid, in_specs=in_specs, out_specs=query_spec...  6.28 us
    unnamed x27, local copies, waits for them, and re-layouts  5.21 us
  transfers between devices with their start and end apart: 8, of which 5 were waited for; matrix products, arithmetic and copies ran while one was open for 10% of the time, Pallas kernels for 4%

profile of v1, /device:TPU:6, one launch (start us, length us, event | category | flops | bytes accessed | tf_op | source)
XLA Modules:
  0.0 177.2 jit_solution(15166769170965782785)
XLA Ops:
  7.2 0.0 copy-start
  7.2 0.0 all-gather.2.cloned.1.call-start
  7.2 0.7 all-gather.2.cloned.1.call-update
  8.0 0.2 convert_reduce_fusion.1
  8.1 0.1 select_reduce_fusion.1
  8.2 0.7 copy.47
  8.9 12.8 %all-to-all-start.1 = ((s32[64,1,1]{2,1,0:T(1,128)}), s32[64,1,1]{2,1,0:T(1,128)}, u32[]{:S(2)}, u32[]{:S(2)}) async-start(s32[64,1,1]{2,1,0:T(1,128)} %copy.47), calls=%async_computation.1 | async-start | bytes 65536 | tf_op jit(solution)/shard_map/all_to_all | solution.py:165
  21.8 0.0 copy-start.9
  21.8 0.6 copy-done.9
  22.4 0.1 copy.41
  22.6 0.1 multiply_reduce_fusion
  22.7 0.1 fusion.1
  22.8 1.2 multiply_cosine_fusion
  24.0 25.2 %all-gather.2.cloned.1.call-done = bf16[256,2048]{1,0:T(8,128)(2,1)} async-done(((bf16[256,256]{1,0:T(8,128)(2,1)}), bf16[256,2048]{1,0:T(8,128)(2,1)}) %all-gather.2.cloned.1.call-update) | async-done | bytes 1048592 | tf_op jit(solution)/shard_map/all_gather | solution.py:125
  49.2 1.7 fusion.8
  51.0 0.1 copy.50
  51.2 0.0 copy-start.6
  51.2 0.8 copy.51
  52.0 1.3 subtract_convert_fusion
  53.3 0.4 pad_maximum_fusion.2
  53.7 0.4 convolution_convert_fusion
  54.2 0.0 copy-start.3
  54.2 0.1 reshape.321
  54.3 1.6 gather_fusion
  55.9 10.4 %all-to-all-start = ((bf16[64,16,2,256]{3,1,2,0:T(8,128)(2,1)}), bf16[64,16,2,256]{3,1,2,0:T(8,128)(2,1)S(1)}, u32[]{:S(2)}, u32[]{:S(2)}) async-start(bf16[64,16,2,256]{3,1,2,0:T(8,128)(2,1)} %gather_fusion), calls=%async_computation | async-start | bytes 2097152 | tf_op jit(solution)/shard_map/all_to_all | solution.py:164
  66.4 3.4 %collective-permute-start = (bf16[256,512]{1,0:T(8,128)(2,1)S(1)}, bf16[256,512]{1,0:T(8,128)(2,1)S(1)}, u32[]{:S(2)}, u32[]{:S(2)}) collective-permute-start(bf16[256,512]{1,0:T(8,128)(2,1)S(1)} %pad_maximum_fusion.1.refs_0_.refs_7_), channel_id=1, source_target_pairs={{0,8},{8,16},{16,24},{24,32},{32,40},{40,48},{48,56},{56,64},{64,7... | collective-permute-start | bytes 786440 | tf_op jit(solution)/shard_map/ppermute | solution.py:20
  69.8 6.4 %collective-permute-start.1 = (bf16[256,512]{1,0:T(8,128)(2,1)S(1)}, bf16[256,512]{1,0:T(8,128)(2,1)S(1)}, u32[]{:S(2)}, u32[]{:S(2)}) collective-permute-start(bf16[256,512]{1,0:T(8,128)(2,1)S(1)} %pad_maximum_fusion.1.refs_0_.refs_7_), channel_id=1, source_target_pairs={{0,24},{8,32},{16,40},{24,48},{32,56},{40,64},{48,72},{56,80},{64,... | collective-permute-start | bytes 786440 | tf_op jit(solution)/shard_map/ppermute | solution.py:20
  76.2 0.1 broadcast_subtract_fusion
  76.3 0.1 convert_reduce_fusion
  76.4 25.0 %collective-permute-done.refs_1_.refs_8_ = bf16[256,512]{1,0:T(8,128)(2,1)S(1)} collective-permute-done((bf16[256,512]{1,0:T(8,128)(2,1)S(1)}, bf16[256,512]{1,0:T(8,128)(2,1)S(1)}, u32[]{:S(2)}, u32[]{:S(2)}) %collective-permute-start) | collective-permute-done | bytes 262176 | tf_op jit(solution)/shard_map/ppermute | solution.py:20
  101.4 14.7 %collective-permute-done.1.refs_3_.refs_10_ = bf16[256,512]{1,0:T(8,128)(2,1)S(1)} collective-permute-done((bf16[256,512]{1,0:T(8,128)(2,1)S(1)}, bf16[256,512]{1,0:T(8,128)(2,1)S(1)}, u32[]{:S(2)}, u32[]{:S(2)}) %collective-permute-start.1) | collective-permute-done | bytes 262176 | tf_op jit(solution)/shard_map/ppermute | solution.py:20
  116.1 0.9 pad_maximum_fusion
  117.0 2.7 %collective-permute-start.2 = (bf16[256,1024]{1,0:T(8,128)(2,1)}, bf16[256,1024]{1,0:T(8,128)(2,1)S(1)}, u32[]{:S(2)}, u32[]{:S(2)}) collective-permute-start(bf16[256,1024]{1,0:T(8,128)(2,1)} %pad_maximum_fusion), channel_id=1, source_target_pairs={{0,8},{8,16},{16,24},{24,32},{32,40},{40,48},{48,56},{56,64},{64,7... | collective-permute-start | bytes 1572872 | tf_op jit(solution)/shard_map/ppermute | solution.py:20
  119.7 0.7 compare_select_fusion.1.key_segment_ref
  120.3 0.8 copy.45.query_segment_ref
  121.1 1.7 copy.52
  122.8 2.0 %reduce.3 = s32[64]{0:T(128)S(1)} reduce(s32[64,1,1]{2,1,0:T(1,128)} %all-to-all-done.1, s32[]{:T(128)} %constant.26.clone.1), dimensions={1,2}, to_apply=%all_to_all.8.reduce_sub_computation | reduce | bytes 516 | tf_op jit(solution)/shard_map/all_to_all | solution.py:165
  124.8 0.1 select_reduce_fusion
  124.9 3.0 %collective-permute-start.3 = (bf16[256,512]{1,0:T(8,128)(2,1)S(1)}, bf16[256,512]{1,0:T(8,128)(2,1)S(1)}, u32[]{:S(2)}, u32[]{:S(2)}) collective-permute-start(bf16[256,512]{1,0:T(8,128)(2,1)S(1)} %pad_maximum_fusion.1.refs_0_.refs_7_), channel_id=1, source_target_pairs={{0,40},{8,48},{16,56},{24,64},{32,72},{40,80},{48,88},{56,96},{64,... | collective-permute-start | bytes 786440 | tf_op jit(solution)/shard_map/ppermute | solution.py:20
  127.9 3.1 %collective-permute-start.4 = (bf16[256,512]{1,0:T(8,128)(2,1)S(1)}, bf16[256,512]{1,0:T(8,128)(2,1)S(1)}, u32[]{:S(2)}, u32[]{:S(2)}) collective-permute-start(bf16[256,512]{1,0:T(8,128)(2,1)S(1)} %pad_maximum_fusion.1.refs_0_.refs_7_), channel_id=1, source_target_pairs={{0,48},{8,56},{16,64},{24,72},{32,80},{40,88},{48,96},{56,104},{64... | collective-permute-start | bytes 786440 | tf_op jit(solution)/shard_map/ppermute | solution.py:20
  131.1 17.5 %collective-permute-done.3.refs_5_.refs_12_ = bf16[256,512]{1,0:T(8,128)(2,1)S(1)} collective-permute-done((bf16[256,512]{1,0:T(8,128)(2,1)S(1)}, bf16[256,512]{1,0:T(8,128)(2,1)S(1)}, u32[]{:S(2)}, u32[]{:S(2)}) %collective-permute-start.3) | collective-permute-done | bytes 262176 | tf_op jit(solution)/shard_map/ppermute | solution.py:20
  148.5 11.4 %collective-permute-done.4.refs_6_.refs_13_ = bf16[256,512]{1,0:T(8,128)(2,1)S(1)} collective-permute-done((bf16[256,512]{1,0:T(8,128)(2,1)S(1)}, bf16[256,512]{1,0:T(8,128)(2,1)S(1)}, u32[]{:S(2)}, u32[]{:S(2)}) %collective-permute-start.4) | collective-permute-done | bytes 262176 | tf_op jit(solution)/shard_map/ppermute | solution.py:20
  159.9 0.7 copy-done.8
  160.6 0.2 copy-done.1
  160.8 6.3 %block_attention.1 = bf16[256,512]{1,0:T(8,128)(2,1)} custom-call(s32[256,1]{1,0:T(8,128)} %copy.45.query_segment_ref, s32[7,256]{1,0:T(8,128)} %compare_select_fusion.1.key_segment_ref, bf16[256,512]{1,0:T(8,128)(2,1)} %bitcast.24, bf16[256,512]{1,0:T(8,128)(2,1)} %copy-done.3, bf16[256,512]{1,0:T(8,128)(2,1)} %copy-done.4, bf16[256,1024]{1,0:T(8,128)(2,1)} %copy-done.1, ...), custom_call_target="tpu_custom_call" | custom-call | flops 1409286144 | bytes 2359296 | tf_op jit(solution)/shard_map/block_attention/pallas_call | solution.py:106
  167.1 1.7 reshape.320
  168.8 0.6 gather_fusion.1
  169.4 0.9 copy.48
  (36 shorter events, 0.2 us)
Async XLA Ops:
  7.2 42.1 %copy-start = (bf16[2048,256]{1,0:T(8,128)(2,1)S(1)}, bf16[2048,256]{1,0:T(8,128)(2,1)}, u32[]{:S(2)}) copy-start(bf16[2048,256]{1,0:T(8,128)(2,1)} %param.7) | copy-start | bytes 3145732
  7.2 0.7 copy-start.10
  7.2 42.0 %all-gather.2.cloned.1.call-start = ((), (), s32[]{:S(2)}) async-start(), calls=%async_computation.2 | async-start | bytes 1179648 | tf_op jit(solution)/shard_map/all_gather | solution.py:125
  8.9 47.0 %all-to-all-start.1 = ((s32[64,1,1]{2,1,0:T(1,128)}), s32[64,1,1]{2,1,0:T(1,128)}, u32[]{:S(2)}, u32[]{:S(2)}) async-start(s32[64,1,1]{2,1,0:T(1,128)} %copy.47), calls=%async_computation.1 | async-start | bytes 65536 | tf_op jit(solution)/shard_map/all_to_all | solution.py:165
  21.8 0.7 copy-start.9
  51.2 2.6 %copy-start.2 = (bf16[256,2048]{1,0:T(8,128)(2,1)S(1)}, bf16[256,2048]{1,0:T(8,128)(2,1)}, u32[]{:S(2)}) copy-start(bf16[256,2048]{1,0:T(8,128)(2,1)} %all-gather.2.cloned.1.call-done) | copy-start | bytes 3145732
  51.2 2.6 %copy-start.6 = (bf16[2048,256]{1,0:T(8,128)(2,1)S(1)}, bf16[2048,256]{1,0:T(8,128)(2,1)}, u32[]{:S(2)}) copy-start(bf16[2048,256]{1,0:T(8,128)(2,1)} %param.8) | copy-start | bytes 3145732
  54.2 73.7 %copy-start.3 = (bf16[256,512]{1,0:T(8,128)(2,1)}, bf16[256,512]{1,0:T(8,128)(2,1)S(1)}, u32[]{:S(2)}) copy-start(bf16[256,512]{1,0:T(8,128)(2,1)S(1)} %pad_maximum_fusion.1.refs_0_.refs_7_) | copy-start | bytes 786436
  55.9 112.9 %all-to-all-start = ((bf16[64,16,2,256]{3,1,2,0:T(8,128)(2,1)}), bf16[64,16,2,256]{3,1,2,0:T(8,128)(2,1)S(1)}, u32[]{:S(2)}, u32[]{:S(2)}) async-start(bf16[64,16,2,256]{3,1,2,0:T(8,128)(2,1)} %gather_fusion), calls=%async_computation | async-start | bytes 2097152 | tf_op jit(solution)/shard_map/all_to_all | solution.py:164
  66.4 35.0 %collective-permute-start = (bf16[256,512]{1,0:T(8,128)(2,1)S(1)}, bf16[256,512]{1,0:T(8,128)(2,1)S(1)}, u32[]{:S(2)}, u32[]{:S(2)}) collective-permute-start(bf16[256,512]{1,0:T(8,128)(2,1)S(1)} %pad_maximum_fusion.1.refs_0_.refs_7_), channel_id=1, source_target_pairs={{0,8},{8,16},{16,24},{24,32},{32,40},{40,48},{48,56},{56,64},{64,7... | collective-permute-start | bytes 786440 | tf_op jit(solution)/shard_map/ppermute | solution.py:20
  69.8 46.3 %collective-permute-start.1 = (bf16[256,512]{1,0:T(8,128)(2,1)S(1)}, bf16[256,512]{1,0:T(8,128)(2,1)S(1)}, u32[]{:S(2)}, u32[]{:S(2)}) collective-permute-start(bf16[256,512]{1,0:T(8,128)(2,1)S(1)} %pad_maximum_fusion.1.refs_0_.refs_7_), channel_id=1, source_target_pairs={{0,24},{8,32},{16,40},{24,48},{32,56},{40,64},{48,72},{56,80},{64,... | collective-permute-start | bytes 786440 | tf_op jit(solution)/shard_map/ppermute | solution.py:20
  101.4 15.6 %copy-start.4 = (bf16[256,512]{1,0:T(8,128)(2,1)}, bf16[256,512]{1,0:T(8,128)(2,1)S(1)}, u32[]{:S(2)}) copy-start(bf16[256,512]{1,0:T(8,128)(2,1)S(1)} %collective-permute-done.refs_1_.refs_8_) | copy-start | bytes 786436
  116.1 0.9 copy-start.5
  117.0 42.9 %collective-permute-start.2 = (bf16[256,1024]{1,0:T(8,128)(2,1)}, bf16[256,1024]{1,0:T(8,128)(2,1)S(1)}, u32[]{:S(2)}, u32[]{:S(2)}) collective-permute-start(bf16[256,1024]{1,0:T(8,128)(2,1)} %pad_maximum_fusion), channel_id=1, source_target_pairs={{0,8},{8,16},{16,24},{24,32},{32,40},{40,48},{48,56},{56,64},{64,7... | collective-permute-start | bytes 1572872 | tf_op jit(solution)/shard_map/ppermute | solution.py:20
  124.9 23.6 %collective-permute-start.3 = (bf16[256,512]{1,0:T(8,128)(2,1)S(1)}, bf16[256,512]{1,0:T(8,128)(2,1)S(1)}, u32[]{:S(2)}, u32[]{:S(2)}) collective-permute-start(bf16[256,512]{1,0:T(8,128)(2,1)S(1)} %pad_maximum_fusion.1.refs_0_.refs_7_), channel_id=1, source_target_pairs={{0,40},{8,48},{16,56},{24,64},{32,72},{40,80},{48,88},{56,96},{64,... | collective-permute-start | bytes 786440 | tf_op jit(solution)/shard_map/ppermute | solution.py:20
  127.9 32.0 %collective-permute-start.4 = (bf16[256,512]{1,0:T(8,128)(2,1)S(1)}, bf16[256,512]{1,0:T(8,128)(2,1)S(1)}, u32[]{:S(2)}, u32[]{:S(2)}) collective-permute-start(bf16[256,512]{1,0:T(8,128)(2,1)S(1)} %pad_maximum_fusion.1.refs_0_.refs_7_), channel_id=1, source_target_pairs={{0,48},{8,56},{16,64},{24,72},{32,80},{40,88},{48,96},{56,104},{64... | collective-permute-start | bytes 786440 | tf_op jit(solution)/shard_map/ppermute | solution.py:20
  148.5 11.4 %copy-start.7 = (bf16[256,512]{1,0:T(8,128)(2,1)}, bf16[256,512]{1,0:T(8,128)(2,1)S(1)}, u32[]{:S(2)}) copy-start(bf16[256,512]{1,0:T(8,128)(2,1)S(1)} %collective-permute-done.3.refs_5_.refs_12_) | copy-start | bytes 786436
  159.9 0.7 copy-start.8
  159.9 0.9 copy-start.1
Sparse Core Ops, SparseCore 0:
  10.1 39.0 all-gather.1

commit v2 on v1

--- a/solution.py
+++ b/solution.py
@@ -122,7 +122,9 @@
     first_row = lax.axis_index("seq") * block_rows
     positions = first_row + jnp.arange(block_rows, dtype=jnp.int32)
     segment, offsets = segment_info(positions, prompt_pages)
-    piece = lax.all_gather(tokens, "tp", axis=1, tiled=True)
+    own = tokens.reshape(block_rows, 1, 1, tokens.shape[1])
+    across = lax.all_gather(own, "zhi", axis=1, tiled=True)
+    piece = lax.all_gather(across, "core", axis=2, tiled=True).reshape(block_rows, -1)
     raw_keys = jnp.dot(piece, key_weight, preferred_element_type=jnp.float32)
     raw_values = jnp.dot(piece, value_weight, preferred_element_type=jnp.float32)
     keys = rotate_heads(raw_keys.reshape(block_rows, local_heads, HD), offsets).astype(jnp.bfloat16)
@@ -172,6 +174,9 @@
 
 
 def solution(mesh):
-    in_specs = (P("seq", "tp"), P(None, "tp"), P(None, "tp"), P("seq", None, "tp"), P(), P("seq"))
-    out_specs = (P("seq", None, "tp"), P("seq", None, None, "tp"))
-    return jax.shard_map(body, mesh=mesh, in_specs=in_specs, out_specs=out_specs, check_vma=False)
+    seq, tp = mesh.devices.shape
+    chips = jax.sharding.Mesh(mesh.devices.reshape(seq, tp // 2, 2), ("seq", "zhi", "core"))
+    heads = ("zhi", "core")
+    in_specs = (P("seq", heads), P(None, heads), P(None, heads), P("seq", None, heads), P(), P("seq"))
+    out_specs = (P("seq", None, heads), P("seq", None, None, heads))
+    return jax.shard_map(body, mesh=chips, in_specs=in_specs, out_specs=out_specs, check_vma=False)

time: 178 us -> 183 us (1.028)
  waiting for transfers between devices: 94.4 us -> 71.4 us
  blocking collectives: 0 us -> 21.8 us
  local copies, waits for them, and re-layouts: 10.8 us -> 19.8 us
  other arithmetic: 7.36 us -> 4.05 us
    all_gather x1, waiting for transfers between devices: 25.2 us -> 2.7 us  [body(): lax.all_gather(across, 'core', axis=2, tiled=True).reshape(block_rows, -1)]
    all_gather x0 -> x1, blocking collectives: none -> 21.8 us  [body(): across = lax.all_gather(own, 'zhi', axis=1, tiled=True)]
    all_gather x0 -> x2, local copies, waits for them, and re-layouts: none -> 3.33 us  [the longest x1 2.3 us: body(): lax.all_gather(across, 'core', axis=2, tiled=True).reshape(block_rows, -1)]
    reshape x0 -> x2, local copies, waits for them, and re-layouts: none -> 3.23 us  [body(): lax.all_gather(across, 'core', axis=2, tiled=True).reshape(block_rows, -1)]
    unnamed x27 -> x25, local copies, waits for them, and re-layouts: 5.21 us -> 6.95 us
  transfers between devices with their start and end apart: 8 -> 8, of which waited for: 5 -> 5; matrix products, arithmetic and copies ran while one was open for 10% -> 11% of each run, Pallas kernels for 4% -> 3%
where the time goes in v2:
time: 183 us; the launch traced here: 182 us
  waiting for transfers between devices  71.4 us (39%)
  starting transfers between devices  42 us (23%)
  blocking collectives  21.8 us (12%)
  local copies, waits for them, and re-layouts  19.8 us (11%)
  between operations  14.3 us (8%)
  Pallas kernels  6.28 us (3%)
  other arithmetic  4.05 us (2%)
  matrix products  2.13 us (1%)
    ppermute x5, waiting for transfers between devices, from_behind(): return lax.ppermute(value, axis, pairs)  68.7 us
    all_gather x1, blocking collectives, body(): across = lax.all_gather(own, 'zhi', axis=1, tiled=True)  21.8 us
    ppermute x5, starting transfers between devices, from_behind(): return lax.ppermute(value, axis, pairs)  18.5 us
    all_to_all x1, starting transfers between devices, body(): lax.all_to_all(labels, 'seq', split_axis=0, concat_axis=0, tiled=True)  11.9 us
    all_to_all x1, starting transfers between devices, body(): lax.all_to_all(outgoing, 'seq', split_axis=0, concat_axis=0, tiled=True)  11.5 us
    unnamed x25, local copies, waits for them, and re-layouts  6.95 us
    pallas_call x1, Pallas kernels, attend(): pl.pallas_call(kernel, grid=grid, in_specs=in_specs, out_specs=query_spec...  6.28 us
  transfers between devices with their start and end apart: 8, of which 5 were waited for; matrix products, arithmetic and copies ran while one was open for 11% of the time, Pallas kernels for 3%

profile of v2, /device:TPU:6, one launch (start us, length us, event | category | flops | bytes accessed | tf_op | source)
XLA Modules:
  0.0 181.8 jit_solution(13013118216849772264)
XLA Ops:
  7.2 1.1 copy.49
  8.3 21.8 %all-gather = bf16[256,1024]{0,1:T(8,128)(2,1)S(1)} all-gather(bf16[256,256]{0,1:T(8,128)(2,1)S(1)} %copy.49), channel_id=2, replica_groups=mesh['seq'=64,'zhi'=4,'core'=2] {'zhi'}, dimensions={1}, use_global_device_ids=true | all-gather | bytes 655360 | tf_op jit(solution)/shard_map/all_gather | solution.py:126
  30.2 1.0 copy.50
  31.2 0.6 copy-done.10
  31.9 0.2 convert_reduce_fusion.1
  32.1 0.1 select_reduce_fusion.1
  32.2 0.7 copy.57
  32.9 11.9 %all-to-all-start.1 = ((s32[64,1,1]{2,1,0:T(1,128)}), s32[64,1,1]{2,1,0:T(1,128)S(1)}, u32[]{:S(2)}, u32[]{:S(2)}) async-start(s32[64,1,1]{2,1,0:T(1,128)} %copy.57), calls=%async_computation.1 | async-start | bytes 65536 | tf_op jit(solution)/shard_map/all_to_all | solution.py:167
  44.8 0.6 copy-done.9
  45.5 0.1 copy.48
  45.6 0.6 copy.60
  46.3 0.1 multiply_reduce_fusion
  46.4 0.1 fusion.1
  46.5 0.3 multiply_cosine_fusion
  46.8 2.7 %all-gather.3.cloned.1.call-done = bf16[256,4,2,256]{3,0,1,2:T(8,128)(2,1)} async-done(((bf16[256,4,1,256]{3,0,1,2:T(8,128)(2,1)}), bf16[256,4,2,256]{3,0,1,2:T(8,128)(2,1)}) %all-gather.3.cloned.1.call-update) | async-done | bytes 1048592 | tf_op jit(solution)/shard_map/all_gather | solution.py:127
  49.5 2.3 %copy.51 = bf16[256,4,2,256]{3,2,1,0:T(2,128)(2,1)S(1)} copy(bf16[256,4,2,256]{3,0,1,2:T(8,128)(2,1)} %all-gather.3.cloned.1.call-done) | data formatting | bytes 2097152 | tf_op jit(solution)/shard_map/all_gather | solution.py:127
  51.8 1.6 reshape.325
  53.4 1.6 reshape.345
  55.0 1.7 fusion.7
  56.8 0.1 copy.61
  56.9 1.0 copy-done.2
  58.0 0.4 convolution_convert_fusion
  58.4 0.1 reshape.327
  58.5 1.6 gather_fusion
  60.2 11.5 %all-to-all-start = ((bf16[64,16,2,256]{3,1,2,0:T(8,128)(2,1)}), bf16[64,16,2,256]{3,1,2,0:T(8,128)(2,1)S(1)}, u32[]{:S(2)}, u32[]{:S(2)}) async-start(bf16[64,16,2,256]{3,1,2,0:T(8,128)(2,1)} %gather_fusion), calls=%async_computation | async-start | bytes 2097152 | tf_op jit(solution)/shard_map/all_to_all | solution.py:166
  71.7 3.4 %collective-permute-start = (bf16[256,512]{1,0:T(8,128)(2,1)S(1)}, bf16[256,512]{1,0:T(8,128)(2,1)S(1)}, u32[]{:S(2)}, u32[]{:S(2)}) collective-permute-start(bf16[256,512]{1,0:T(8,128)(2,1)S(1)} %pad_maximum_fusion.1.refs_0_.refs_7_), channel_id=1, source_target_pairs={{0,8},{8,16},{16,24},{24,32},{32,40},{40,48},{48,56},{56,64},{64,7... | collective-permute-start | bytes 786440 | tf_op jit(solution)/shard_map/ppermute | solution.py:20
  75.1 6.4 %collective-permute-start.1 = (bf16[256,512]{1,0:T(8,128)(2,1)S(1)}, bf16[256,512]{1,0:T(8,128)(2,1)S(1)}, u32[]{:S(2)}, u32[]{:S(2)}) collective-permute-start(bf16[256,512]{1,0:T(8,128)(2,1)S(1)} %pad_maximum_fusion.1.refs_0_.refs_7_), channel_id=1, source_target_pairs={{0,24},{8,32},{16,40},{24,48},{32,56},{40,64},{48,72},{56,80},{64,... | collective-permute-start | bytes 786440 | tf_op jit(solution)/shard_map/ppermute | solution.py:20
  81.5 0.1 broadcast_subtract_fusion
  81.6 0.1 convert_reduce_fusion
  81.7 24.9 %collective-permute-done.refs_1_.refs_8_ = bf16[256,512]{1,0:T(8,128)(2,1)S(1)} collective-permute-done((bf16[256,512]{1,0:T(8,128)(2,1)S(1)}, bf16[256,512]{1,0:T(8,128)(2,1)S(1)}, u32[]{:S(2)}, u32[]{:S(2)}) %collective-permute-start) | collective-permute-done | bytes 262176 | tf_op jit(solution)/shard_map/ppermute | solution.py:20
  106.6 14.9 %collective-permute-done.1.refs_3_.refs_10_ = bf16[256,512]{1,0:T(8,128)(2,1)S(1)} collective-permute-done((bf16[256,512]{1,0:T(8,128)(2,1)S(1)}, bf16[256,512]{1,0:T(8,128)(2,1)S(1)}, u32[]{:S(2)}, u32[]{:S(2)}) %collective-permute-start.1) | collective-permute-done | bytes 262176 | tf_op jit(solution)/shard_map/ppermute | solution.py:20
  121.5 0.9 pad_maximum_fusion
  122.5 2.6 %collective-permute-start.2 = (bf16[256,1024]{1,0:T(8,128)(2,1)}, bf16[256,1024]{1,0:T(8,128)(2,1)S(1)}, u32[]{:S(2)}, u32[]{:S(2)}) collective-permute-start(bf16[256,1024]{1,0:T(8,128)(2,1)} %pad_maximum_fusion), channel_id=1, source_target_pairs={{0,8},{8,16},{16,24},{24,32},{32,40},{40,48},{48,56},{56,64},{64,7... | collective-permute-start | bytes 1572872 | tf_op jit(solution)/shard_map/ppermute | solution.py:20
  125.1 0.7 compare_select_fusion.1.key_segment_ref
  125.7 0.8 copy.55.query_segment_ref
  126.5 1.7 copy.62
  128.2 1.2 reduce.3
  129.4 0.1 select_reduce_fusion
  129.5 3.0 %collective-permute-start.3 = (bf16[256,512]{1,0:T(8,128)(2,1)S(1)}, bf16[256,512]{1,0:T(8,128)(2,1)S(1)}, u32[]{:S(2)}, u32[]{:S(2)}) collective-permute-start(bf16[256,512]{1,0:T(8,128)(2,1)S(1)} %pad_maximum_fusion.1.refs_0_.refs_7_), channel_id=1, source_target_pairs={{0,40},{8,48},{16,56},{24,64},{32,72},{40,80},{48,88},{56,96},{64,... | collective-permute-start | bytes 786440 | tf_op jit(solution)/shard_map/ppermute | solution.py:20
  132.5 3.1 %collective-permute-start.4 = (bf16[256,512]{1,0:T(8,128)(2,1)S(1)}, bf16[256,512]{1,0:T(8,128)(2,1)S(1)}, u32[]{:S(2)}, u32[]{:S(2)}) collective-permute-start(bf16[256,512]{1,0:T(8,128)(2,1)S(1)} %pad_maximum_fusion.1.refs_0_.refs_7_), channel_id=1, source_target_pairs={{0,48},{8,56},{16,64},{24,72},{32,80},{40,88},{48,96},{56,104},{64... | collective-permute-start | bytes 786440 | tf_op jit(solution)/shard_map/ppermute | solution.py:20
  135.7 17.5 %collective-permute-done.3.refs_5_.refs_12_ = bf16[256,512]{1,0:T(8,128)(2,1)S(1)} collective-permute-done((bf16[256,512]{1,0:T(8,128)(2,1)S(1)}, bf16[256,512]{1,0:T(8,128)(2,1)S(1)}, u32[]{:S(2)}, u32[]{:S(2)}) %collective-permute-start.3) | collective-permute-done | bytes 262176 | tf_op jit(solution)/shard_map/ppermute | solution.py:20
  153.2 11.3 %collective-permute-done.4.refs_6_.refs_13_ = bf16[256,512]{1,0:T(8,128)(2,1)S(1)} collective-permute-done((bf16[256,512]{1,0:T(8,128)(2,1)S(1)}, bf16[256,512]{1,0:T(8,128)(2,1)S(1)}, u32[]{:S(2)}, u32[]{:S(2)}) %collective-permute-start.4) | collective-permute-done | bytes 262176 | tf_op jit(solution)/shard_map/ppermute | solution.py:20
  164.6 0.7 copy-done.8
  165.3 0.2 copy-done.1
  165.5 6.3 %block_attention.1 = bf16[256,512]{1,0:T(8,128)(2,1)} custom-call(s32[256,1]{1,0:T(8,128)} %copy.55.query_segment_ref, s32[7,256]{1,0:T(8,128)} %compare_select_fusion.1.key_segment_ref, bf16[256,512]{1,0:T(8,128)(2,1)} %bitcast.25, bf16[256,512]{1,0:T(8,128)(2,1)} %copy-done.3, bf16[256,512]{1,0:T(8,128)(2,1)} %copy-done.4, bf16[256,1024]{1,0:T(8,128)(2,1)} %copy-done.1, ...), custom_call_target="tpu_custom_call" | custom-call | flops 1409286144 | bytes 2359296 | tf_op jit(solution)/shard_map/block_attention/pallas_call | solution.py:106
  171.8 1.7 reshape.326
  173.5 0.6 gather_fusion.1
  174.1 0.9 copy.58
  (40 shorter events, 0.3 us)
Async XLA Ops:
  7.2 49.7 %copy-start = (bf16[2048,256]{1,0:T(8,128)(2,1)S(1)}, bf16[2048,256]{1,0:T(8,128)(2,1)}, u32[]{:S(2)}) copy-start(bf16[2048,256]{1,0:T(8,128)(2,1)} %param.8) | copy-start | bytes 3145732
  7.2 42.3 %all-gather.3.cloned.1.call-start = ((), (), s32[]{:S(2)}) async-start(), calls=%async_computation.2 | async-start | bytes 1572864 | tf_op jit(solution)/shard_map/all_gather | solution.py:127
  8.3 37.2 %copy-start.6 = (bf16[2048,256]{1,0:T(8,128)(2,1)S(1)}, bf16[2048,256]{1,0:T(8,128)(2,1)}, u32[]{:S(2)}) copy-start(bf16[2048,256]{1,0:T(8,128)(2,1)} %param.7) | copy-start | bytes 3145732
  31.2 0.7 copy-start.10
  32.9 27.3 %all-to-all-start.1 = ((s32[64,1,1]{2,1,0:T(1,128)}), s32[64,1,1]{2,1,0:T(1,128)S(1)}, u32[]{:S(2)}, u32[]{:S(2)}) async-start(s32[64,1,1]{2,1,0:T(1,128)} %copy.57), calls=%async_computation.1 | async-start | bytes 65536 | tf_op jit(solution)/shard_map/all_to_all | solution.py:167
  44.8 0.7 copy-start.9
  56.7 1.2 copy-start.2
  58.4 74.1 %copy-start.3 = (bf16[256,512]{1,0:T(8,128)(2,1)}, bf16[256,512]{1,0:T(8,128)(2,1)S(1)}, u32[]{:S(2)}) copy-start(bf16[256,512]{1,0:T(8,128)(2,1)S(1)} %pad_maximum_fusion.1.refs_0_.refs_7_) | copy-start | bytes 786436
  60.2 113.3 %all-to-all-start = ((bf16[64,16,2,256]{3,1,2,0:T(8,128)(2,1)}), bf16[64,16,2,256]{3,1,2,0:T(8,128)(2,1)S(1)}, u32[]{:S(2)}, u32[]{:S(2)}) async-start(bf16[64,16,2,256]{3,1,2,0:T(8,128)(2,1)} %gather_fusion), calls=%async_computation | async-start | bytes 2097152 | tf_op jit(solution)/shard_map/all_to_all | solution.py:166
  71.7 34.9 %collective-permute-start = (bf16[256,512]{1,0:T(8,128)(2,1)S(1)}, bf16[256,512]{1,0:T(8,128)(2,1)S(1)}, u32[]{:S(2)}, u32[]{:S(2)}) collective-permute-start(bf16[256,512]{1,0:T(8,128)(2,1)S(1)} %pad_maximum_fusion.1.refs_0_.refs_7_), channel_id=1, source_target_pairs={{0,8},{8,16},{16,24},{24,32},{32,40},{40,48},{48,56},{56,64},{64,7... | collective-permute-start | bytes 786440 | tf_op jit(solution)/shard_map/ppermute | solution.py:20
  75.1 46.4 %collective-permute-start.1 = (bf16[256,512]{1,0:T(8,128)(2,1)S(1)}, bf16[256,512]{1,0:T(8,128)(2,1)S(1)}, u32[]{:S(2)}, u32[]{:S(2)}) collective-permute-start(bf16[256,512]{1,0:T(8,128)(2,1)S(1)} %pad_maximum_fusion.1.refs_0_.refs_7_), channel_id=1, source_target_pairs={{0,24},{8,32},{16,40},{24,48},{32,56},{40,64},{48,72},{56,80},{64,... | collective-permute-start | bytes 786440 | tf_op jit(solution)/shard_map/ppermute | solution.py:20
  106.6 15.8 %copy-start.4 = (bf16[256,512]{1,0:T(8,128)(2,1)}, bf16[256,512]{1,0:T(8,128)(2,1)S(1)}, u32[]{:S(2)}) copy-start(bf16[256,512]{1,0:T(8,128)(2,1)S(1)} %collective-permute-done.refs_1_.refs_8_) | copy-start | bytes 786436
  121.5 0.9 copy-start.5
  122.5 42.1 %collective-permute-start.2 = (bf16[256,1024]{1,0:T(8,128)(2,1)}, bf16[256,1024]{1,0:T(8,128)(2,1)S(1)}, u32[]{:S(2)}, u32[]{:S(2)}) collective-permute-start(bf16[256,1024]{1,0:T(8,128)(2,1)} %pad_maximum_fusion), channel_id=1, source_target_pairs={{0,8},{8,16},{16,24},{24,32},{32,40},{40,48},{48,56},{56,64},{64,7... | collective-permute-start | bytes 1572872 | tf_op jit(solution)/shard_map/ppermute | solution.py:20
  129.5 23.7 %collective-permute-start.3 = (bf16[256,512]{1,0:T(8,128)(2,1)S(1)}, bf16[256,512]{1,0:T(8,128)(2,1)S(1)}, u32[]{:S(2)}, u32[]{:S(2)}) collective-permute-start(bf16[256,512]{1,0:T(8,128)(2,1)S(1)} %pad_maximum_fusion.1.refs_0_.refs_7_), channel_id=1, source_target_pairs={{0,40},{8,48},{16,56},{24,64},{32,72},{40,80},{48,88},{56,96},{64,... | collective-permute-start | bytes 786440 | tf_op jit(solution)/shard_map/ppermute | solution.py:20
  132.5 32.1 %collective-permute-start.4 = (bf16[256,512]{1,0:T(8,128)(2,1)S(1)}, bf16[256,512]{1,0:T(8,128)(2,1)S(1)}, u32[]{:S(2)}, u32[]{:S(2)}) collective-permute-start(bf16[256,512]{1,0:T(8,128)(2,1)S(1)} %pad_maximum_fusion.1.refs_0_.refs_7_), channel_id=1, source_target_pairs={{0,48},{8,56},{16,64},{24,72},{32,80},{40,88},{48,96},{56,104},{64... | collective-permute-start | bytes 786440 | tf_op jit(solution)/shard_map/ppermute | solution.py:20
  153.2 11.4 %copy-start.7 = (bf16[256,512]{1,0:T(8,128)(2,1)}, bf16[256,512]{1,0:T(8,128)(2,1)S(1)}, u32[]{:S(2)}) copy-start(bf16[256,512]{1,0:T(8,128)(2,1)S(1)} %collective-permute-done.3.refs_5_.refs_12_) | copy-start | bytes 786436
  164.6 0.7 copy-start.8
  164.6 0.9 copy-start.1
Sparse Core Ops, SparseCore 0:
  31.3 18.1 all-gather.2

commit v3 on v1

--- a/solution.py
+++ b/solution.py
@@ -39,79 +39,131 @@
     return jnp.concatenate([lower * cosine - upper * sine, upper * cosine + lower * sine], axis=-1)
 
 
-def attention_kernel(query_segment_ref, key_segment_ref, query_ref, *refs, blocks, scale):
+def masked_scores(query, query_segment, key_segment_ref, key_ref, slot, diagonal, scale):
+    rows = query.shape[0]
+    product = lax.dot_general(
+        query, key_ref[...], (((1,), (1,)), ((), ())), preferred_element_type=jnp.float32
+    )
+    allowed = query_segment == key_segment_ref[pl.ds(slot, 1), :]
+    if diagonal:
+        row = lax.broadcasted_iota(jnp.int32, (rows, rows), 0)
+        col = lax.broadcasted_iota(jnp.int32, (rows, rows), 1)
+        allowed = allowed & (col <= row)
+    return jnp.where(allowed, product * scale, -jnp.inf)
+
+
+def accumulate(scores, value_refs, peak, total, summed):
+    for slot, value_ref in enumerate(value_refs):
+        weight = jnp.exp(scores(slot) - peak)
+        total = total + jnp.sum(weight, axis=1, keepdims=True)
+        summed = summed + jnp.dot(
+            weight.astype(jnp.bfloat16), value_ref[...], preferred_element_type=jnp.float32
+        )
+    return total, summed
+
+
+def first_kernel(query_segment_ref, key_segment_ref, query_ref, *refs, blocks, scale):
+    key_refs = refs[:blocks]
+    value_refs = refs[blocks : 2 * blocks]
+    peak_ref, total_ref, summed_ref = refs[2 * blocks :]
+    query = query_ref[...]
+    query_segment = query_segment_ref[...]
+
+    def scores(slot):
+        return masked_scores(
+            query, query_segment, key_segment_ref, key_refs[slot], slot, slot == 0, scale
+        )
+
+    peak = jnp.max(scores(0), axis=1, keepdims=True)
+    for slot in range(1, blocks):
+        peak = jnp.maximum(peak, jnp.max(scores(slot), axis=1, keepdims=True))
+    total = jnp.zeros(peak.shape, jnp.float32)
+    summed = jnp.zeros(summed_ref.shape, jnp.float32)
+    total, summed = accumulate(scores, value_refs, peak, total, summed)
+    peak_ref[...] = jnp.broadcast_to(peak, peak_ref.shape)
+    total_ref[...] = jnp.broadcast_to(total, total_ref.shape)
+    summed_ref[...] = summed
+
+
+def second_kernel(
+    query_segment_ref, key_segment_ref, query_ref, peak_ref, total_ref, summed_ref, *refs,
+    blocks, scale,
+):
     key_refs = refs[:blocks]
     value_refs = refs[blocks : 2 * blocks]
     out_ref = refs[2 * blocks]
-    rows = query_ref.shape[0]
     query = query_ref[...]
     query_segment = query_segment_ref[...]
-    row = lax.broadcasted_iota(jnp.int32, (rows, rows), 0)
-    col = lax.broadcasted_iota(jnp.int32, (rows, rows), 1)
-
-    def scores(distance):
-        key = key_refs[distance][...]
-        product = lax.dot_general(
-            query, key, (((1,), (1,)), ((), ())), preferred_element_type=jnp.float32
-        )
-        allowed = query_segment == key_segment_ref[pl.ds(distance, 1), :]
-        if distance == 0:
-            allowed = allowed & (col <= row)
-        return jnp.where(allowed, product * scale, -jnp.inf)
-
-    peak = jnp.max(scores(0), axis=1, keepdims=True)
-    for distance in range(1, blocks):
-        peak = jnp.maximum(peak, jnp.max(scores(distance), axis=1, keepdims=True))
-    total = jnp.zeros((rows, 1), jnp.float32)
-    summed = jnp.zeros((rows, out_ref.shape[1]), jnp.float32)
-    for distance in range(blocks):
-        weight = jnp.exp(scores(distance) - peak)
-        total = total + jnp.sum(weight, axis=1, keepdims=True)
-        summed = summed + jnp.dot(
-            weight.astype(jnp.bfloat16),
-            value_refs[distance][...],
-            preferred_element_type=jnp.float32,
-        )
+
+    def scores(slot):
+        return masked_scores(
+            query, query_segment, key_segment_ref, key_refs[slot], slot, False, scale
+        )
+
+    first_peak = peak_ref[:, :1]
+    peak = first_peak
+    for slot in range(blocks):
+        peak = jnp.maximum(peak, jnp.max(scores(slot), axis=1, keepdims=True))
+    factor = jnp.exp(first_peak - peak)
+    total = total_ref[:, :1] * factor
+    summed = summed_ref[...] * factor
+    total, summed = accumulate(scores, value_refs, peak, total, summed)
     out_ref[...] = (summed / total).astype(out_ref.dtype)
 
 
-def attend(query, query_segment, key_segment, sources, local_heads):
+def attend(query, query_segment, key_segment, first, second, local_heads):
     rows = query.shape[0]
-    blocks = len(sources)
     grid = (local_heads, TOPK)
-    query_spec = pl.BlockSpec((rows, HD), lambda h, e: (0, e * local_heads + h))
+    combos = local_heads * TOPK
+    scale = 1.0 / math.sqrt(HD)
+    tile = pl.BlockSpec((rows, HD), lambda h, e: (0, e * local_heads + h))
 
     def column_spec(base):
         return pl.BlockSpec((rows, HD), lambda h, e: (0, base + h))
 
-    key_specs = [column_spec(base) for _, base in sources]
-    value_specs = [column_spec(base + local_heads) for _, base in sources]
-    in_specs = (
-        [
+    def common(sources):
+        specs = [
             pl.BlockSpec((rows, 1), lambda h, e: (0, 0)),
-            pl.BlockSpec((blocks, rows), lambda h, e: (0, 0)),
-            query_spec,
+            pl.BlockSpec((len(sources), rows), lambda h, e: (0, 0)),
+            tile,
         ]
-        + key_specs
-        + value_specs
-    )
-    arrays = [array for array, _ in sources]
-    combos = local_heads * TOPK
-    cost = pl.CostEstimate(
-        flops=combos * 3 * blocks * 2 * rows * rows * HD,
-        transcendentals=combos * blocks * rows * rows,
-        bytes_accessed=2 * query.size * 2 + blocks * rows * 2 * local_heads * HD * 2,
-    )
-    kernel = functools.partial(attention_kernel, blocks=blocks, scale=1.0 / math.sqrt(HD))
+        return specs
+
+    def block_specs(sources):
+        keys = [column_spec(base) for _, base in sources]
+        values = [column_spec(base + local_heads) for _, base in sources]
+        arrays = [array for array, _ in sources]
+        return keys + values, arrays + arrays
+
+    def cost(blocks):
+        return pl.CostEstimate(
+            flops=combos * 3 * blocks * 2 * rows * rows * HD,
+            transcendentals=combos * blocks * rows * rows,
+            bytes_accessed=query.size * 2 + blocks * rows * 2 * local_heads * HD * 2
+            + 3 * combos * rows * HD * 4,
+        )
+
+    stats = jax.ShapeDtypeStruct((rows, combos * HD), jnp.float32)
+    specs, arrays = block_specs(first)
+    peak, total, summed = pl.pallas_call(
+        functools.partial(first_kernel, blocks=len(first), scale=scale),
+        grid=grid,
+        in_specs=common(first) + specs,
+        out_specs=(tile, tile, tile),
+        out_shape=(stats, stats, stats),
+        cost_estimate=cost(len(first)),
+        name="first_blocks",
+    )(query_segment, key_segment[0], query, *arrays)
+    specs, arrays = block_specs(second)
     return pl.pallas_call(
-        kernel,
+        functools.partial(second_kernel, blocks=len(second), scale=scale),
         grid=grid,
-        in_specs=in_specs,
-        out_specs=query_spec,
+        in_specs=common(second) + [tile, tile, tile] + specs,
+        out_specs=tile,
         out_shape=jax.ShapeDtypeStruct(query.shape, jnp.bfloat16),
-        cost_estimate=cost,
-        name="block_attention",
-    )(query_segment, key_segment, query, *arrays, *arrays)
+        cost_estimate=cost(len(second)),
+        name="second_blocks",
+    )(query_segment, key_segment[1], query, peak, total, summed, *arrays)
 
 
 def body(tokens, key_weight, value_weight, queries, prompt_pages, page_table):
@@ -135,17 +187,15 @@
         jnp.concatenate([sent[distance - 1] for distance in relayed], axis=1), "seq", 1
     )
     span = 2 * local_heads
-    sources = [(key_value, 0)]
-    for distance in range(1, BACK + 1):
-        if distance in sent:
-            sources.append((sent[distance], 0))
-        else:
-            sources.append((onward, span * relayed.index(distance)))
-    key_place = positions[None, :] - block_rows * jnp.arange(BACK + 1, dtype=jnp.int32)[:, None]
+    first = [(key_value, 0)] + [(sent[distance], 0) for distance in direct]
+    second = [(onward, span * index) for index in range(len(relayed))]
+    order = [0] + list(direct) + relayed
+    key_place = positions[None, :] - block_rows * jnp.asarray(order, jnp.int32)[:, None]
     key_segment, _ = segment_info(key_place.reshape(-1), prompt_pages)
-    key_segment = jnp.where(key_place >= 0, key_segment.reshape(BACK + 1, block_rows), -1)
+    key_segment = jnp.where(key_place >= 0, key_segment.reshape(len(order), block_rows), -1)
+    key_segment = (key_segment[: len(first)], key_segment[len(first) :])
     query = queries.reshape(block_rows, TOPK * width)
-    attended = attend(query, segment[:, None], key_segment, sources, local_heads)
+    attended = attend(query, segment[:, None], key_segment, first, second, local_heads)
     attended = attended.reshape(block_rows, TOPK, width)
     pages_dev = block_rows // PAGE
     capacity = max(1, pages_dev // devices)

time: 178 us -> 180 us (1.011)
  Pallas kernels: 6.28 us -> 10.6 us
  waiting for transfers between devices: 94.4 us -> 92.2 us
    pallas_call x1 -> x2, Pallas kernels: 6.28 us -> 10.6 us  [the longest x1 5.55 us: attend(): pl.pallas_call(functools.partial(first_kernel, blocks=len(first), scale=s...]
    ppermute x5, waiting for transfers between devices: 68.5 us -> 66.4 us  [from_behind(): return lax.ppermute(value, axis, pairs)]
    unnamed x27 -> x31, local copies, waits for them, and re-layouts: 5.21 us -> 4.89 us
  transfers between devices with their start and end apart: 8 -> 8, of which waited for: 5 -> 5; matrix products, arithmetic and copies ran while one was open for 10% -> 9% of each run, Pallas kernels for 4% -> 6%
where the time goes in v3:
time: 180 us; the launch traced here: 179 us
  waiting for transfers between devices  92.2 us (51%)
  starting transfers between devices  42 us (23%)
  between operations  14.4 us (8%)
  local copies, waits for them, and re-layouts  11 us (6%)
  Pallas kernels  10.6 us (6%)
  other arithmetic  6.84 us (4%)
  matrix products  2.19 us (1%)
    ppermute x5, waiting for transfers between devices, from_behind(): return lax.ppermute(value, axis, pairs)  66.4 us
    all_gather x1, waiting for transfers between devices, body(): piece = lax.all_gather(tokens, 'tp', axis=1, tiled=True)  25.2 us
    ppermute x5, starting transfers between devices, from_behind(): return lax.ppermute(value, axis, pairs)  18.6 us
    all_to_all x1, starting transfers between devices, body(): lax.all_to_all(labels, 'seq', split_axis=0, concat_axis=0, tiled=True)  12.8 us
    all_to_all x1, starting transfers between devices, body(): lax.all_to_all(outgoing, 'seq', split_axis=0, concat_axis=0, tiled=True)  10.6 us
    pallas_call x1, Pallas kernels, attend(): pl.pallas_call(functools.partial(first_kernel, blocks=len(first), scale=s...  5.55 us
    pallas_call x1, Pallas kernels, attend(): pl.pallas_call(functools.partial(second_kernel, blocks=len(second), scale...  5.07 us
    unnamed x31, local copies, waits for them, and re-layouts  4.89 us
  transfers between devices with their start and end apart: 8, of which 5 were waited for; matrix products, arithmetic and copies ran while one was open for 9% of the time, Pallas kernels for 6%

profile of v3, /device:TPU:6, one launch (start us, length us, event | category | flops | bytes accessed | tf_op | source)
XLA Modules:
  0.0 179.3 jit_solution(17369754744810744371)
XLA Ops:
  7.2 0.0 copy-start
  7.2 0.0 all-gather.2.cloned.1.call-start
  7.2 0.7 all-gather.2.cloned.1.call-update
  8.0 0.2 convert_reduce_fusion.1
  8.1 0.1 select_reduce_fusion.1
  8.2 0.7 copy.53
  9.0 12.8 %all-to-all-start.1 = ((s32[64,1,1]{2,1,0:T(1,128)}), s32[64,1,1]{2,1,0:T(1,128)}, u32[]{:S(2)}, u32[]{:S(2)}) async-start(s32[64,1,1]{2,1,0:T(1,128)} %copy.53), calls=%async_computation.1 | async-start | bytes 65536 | tf_op jit(solution)/shard_map/all_to_all | solution.py:215
  21.8 0.0 copy-start.9
  21.8 0.6 copy-done.9
  22.4 0.1 copy.46
  22.6 0.1 multiply_reduce_fusion
  22.7 0.1 fusion.1
  22.8 1.2 multiply_cosine_fusion
  24.0 25.2 %all-gather.2.cloned.1.call-done = bf16[256,2048]{1,0:T(8,128)(2,1)} async-done(((bf16[256,256]{1,0:T(8,128)(2,1)}), bf16[256,2048]{1,0:T(8,128)(2,1)}) %all-gather.2.cloned.1.call-update) | async-done | bytes 1048592 | tf_op jit(solution)/shard_map/all_gather | solution.py:177
  49.2 1.7 fusion.8
  51.0 0.1 copy.57
  51.2 0.8 copy.56
  52.0 1.3 subtract_convert_fusion
  53.3 0.4 pad_maximum_fusion.2
  53.7 0.4 convolution_convert_fusion
  54.2 0.1 reshape.318
  54.3 1.6 gather_fusion
  55.9 10.6 %all-to-all-start = ((bf16[64,16,2,256]{3,1,2,0:T(8,128)(2,1)}), bf16[64,16,2,256]{3,1,2,0:T(8,128)(2,1)S(1)}, u32[]{:S(2)}, u32[]{:S(2)}) async-start(bf16[64,16,2,256]{3,1,2,0:T(8,128)(2,1)} %gather_fusion), calls=%async_computation | async-start | bytes 2097152 | tf_op jit(solution)/shard_map/all_to_all | solution.py:214
  66.5 0.1 broadcast_add_fusion
  66.6 3.4 %collective-permute-start = (bf16[256,512]{1,0:T(8,128)(2,1)S(1)}, bf16[256,512]{1,0:T(8,128)(2,1)S(1)}, u32[]{:S(2)}, u32[]{:S(2)}) collective-permute-start(bf16[256,512]{1,0:T(8,128)(2,1)S(1)} %pad_maximum_fusion.1.refs_0_.refs_5_), channel_id=1, source_target_pairs={{0,8},{8,16},{16,24},{24,32},{32,40},{40,48},{48,56},{56,64},{64,7... | collective-permute-start | bytes 786440 | tf_op jit(solution)/shard_map/ppermute | solution.py:20
  70.0 6.4 %collective-permute-start.1 = (bf16[256,512]{1,0:T(8,128)(2,1)S(1)}, bf16[256,512]{1,0:T(8,128)(2,1)}, u32[]{:S(2)}, u32[]{:S(2)}) collective-permute-start(bf16[256,512]{1,0:T(8,128)(2,1)S(1)} %pad_maximum_fusion.1.refs_0_.refs_5_), channel_id=1, source_target_pairs={{0,24},{8,32},{16,40},{24,48},{32,56},{40,64},{48,72},{56,80},{64,... | collective-permute-start | bytes 786440 | tf_op jit(solution)/shard_map/ppermute | solution.py:20
  76.4 0.1 convert_reduce_fusion
  76.5 0.8 copy.51.query_segment_ref
  77.3 0.1 compare_select_fusion.1
  77.4 0.6 slice.20.key_segment_ref
  78.0 0.7 copy.58
  78.7 2.0 %reduce.3 = s32[64]{0:T(128)S(1)} reduce(s32[64,1,1]{2,1,0:T(1,128)} %all-to-all-done.1, s32[]{:T(128)} %constant.27.clone.1), dimensions={1,2}, to_apply=%all_to_all.8.reduce_sub_computation | reduce | bytes 516 | tf_op jit(solution)/shard_map/all_to_all | solution.py:215
  80.7 20.9 %collective-permute-done.refs_1_.refs_6_ = bf16[256,512]{1,0:T(8,128)(2,1)S(1)} collective-permute-done((bf16[256,512]{1,0:T(8,128)(2,1)S(1)}, bf16[256,512]{1,0:T(8,128)(2,1)S(1)}, u32[]{:S(2)}, u32[]{:S(2)}) %collective-permute-start) | collective-permute-done | bytes 262176 | tf_op jit(solution)/shard_map/ppermute | solution.py:20
  101.5 14.8 %collective-permute-done.1.refs_2_.refs_7_ = bf16[256,512]{1,0:T(8,128)(2,1)} collective-permute-done((bf16[256,512]{1,0:T(8,128)(2,1)S(1)}, bf16[256,512]{1,0:T(8,128)(2,1)}, u32[]{:S(2)}, u32[]{:S(2)}) %collective-permute-start.1) | collective-permute-done | bytes 262176 | tf_op jit(solution)/shard_map/ppermute | solution.py:20
  116.3 1.0 pad_maximum_fusion
  117.3 2.7 %collective-permute-start.4 = (bf16[256,1024]{1,0:T(8,128)(2,1)S(1)}, bf16[256,1024]{1,0:T(8,128)(2,1)S(1)}, u32[]{:S(2)}, u32[]{:S(2)}) collective-permute-start(bf16[256,1024]{1,0:T(8,128)(2,1)S(1)} %pad_maximum_fusion), channel_id=1, source_target_pairs={{0,8},{8,16},{16,24},{24,32},{32,40},{40,48},{48,56},{56,64},{64,7... | collective-permute-start | bytes 1572872 | tf_op jit(solution)/shard_map/ppermute | solution.py:20
  120.0 0.1 select_reduce_fusion
  120.1 3.0 %collective-permute-start.2 = (bf16[256,512]{1,0:T(8,128)(2,1)S(1)}, bf16[256,512]{1,0:T(8,128)(2,1)S(1)}, u32[]{:S(2)}, u32[]{:S(2)}) collective-permute-start(bf16[256,512]{1,0:T(8,128)(2,1)S(1)} %pad_maximum_fusion.1.refs_0_.refs_5_), channel_id=1, source_target_pairs={{0,40},{8,48},{16,56},{24,64},{32,72},{40,80},{48,88},{56,96},{64,... | collective-permute-start | bytes 786440 | tf_op jit(solution)/shard_map/ppermute | solution.py:20
  123.1 3.1 %collective-permute-start.3 = (bf16[256,512]{1,0:T(8,128)(2,1)S(1)}, bf16[256,512]{1,0:T(8,128)(2,1)S(1)}, u32[]{:S(2)}, u32[]{:S(2)}) collective-permute-start(bf16[256,512]{1,0:T(8,128)(2,1)S(1)} %pad_maximum_fusion.1.refs_0_.refs_5_), channel_id=1, source_target_pairs={{0,48},{8,56},{16,64},{24,72},{32,80},{40,88},{48,96},{56,104},{64... | collective-permute-start | bytes 786440 | tf_op jit(solution)/shard_map/ppermute | solution.py:20
  126.3 17.5 %collective-permute-done.2.refs_3_.refs_8_ = bf16[256,512]{1,0:T(8,128)(2,1)S(1)} collective-permute-done((bf16[256,512]{1,0:T(8,128)(2,1)S(1)}, bf16[256,512]{1,0:T(8,128)(2,1)S(1)}, u32[]{:S(2)}, u32[]{:S(2)}) %collective-permute-start.2) | collective-permute-done | bytes 262176 | tf_op jit(solution)/shard_map/ppermute | solution.py:20
  143.8 13.2 %collective-permute-done.3.refs_4_.refs_9_ = bf16[256,512]{1,0:T(8,128)(2,1)S(1)} collective-permute-done((bf16[256,512]{1,0:T(8,128)(2,1)S(1)}, bf16[256,512]{1,0:T(8,128)(2,1)S(1)}, u32[]{:S(2)}, u32[]{:S(2)}) %collective-permute-start.3) | collective-permute-done | bytes 262176 | tf_op jit(solution)/shard_map/ppermute | solution.py:20
  157.0 0.7 copy-done.11
  157.8 5.6 %first_blocks.1 = (f32[256,512]{1,0:T(8,128)}, f32[256,512]{1,0:T(8,128)}, f32[256,512]{1,0:T(8,128)}) custom-call(s32[256,1]{1,0:T(8,128)} %copy.51.query_segment_ref, s32[5,256]{1,0:T(8,128)} %bitcast.30, bf16[256,512]{1,0:T(8,128)(2,1)} %bitcast.25, bf16[256,512]{1,0:T(8,128)(2,1)} %copy-done.4, bf16[256,512]{1,0:T(8,128)(2,1)} %copy-done.6, ...), custom_call_target="tpu_custom_call" | custom-call | flops 1006632960 | bytes 3145728 | tf_op jit(solution)/shard_map/first_blocks/pallas_call | solution.py:148
  163.3 0.8 copy-done.1
  164.1 5.1 %second_blocks.1 = bf16[256,512]{1,0:T(8,128)(2,1)} custom-call(s32[256,1]{1,0:T(8,128)} %copy.51.query_segment_ref, s32[2,256]{1,0:T(2,128)} %slice.20.key_segment_ref, bf16[256,512]{1,0:T(8,128)(2,1)} %bitcast.26, f32[256,512]{1,0:T(8,128)} %get-tuple-element.5.peak_ref, f32[256,512]{1,0:T(8,128)} %get-tuple-element.6.total_ref, ...), custom_call_target="tpu_custom_call" | custom-call | flops 402653184 | bytes 2359296 | tf_op jit(solution)/shard_map/second_blocks/pallas_call | solution.py:158
  169.2 1.7 reshape.317
  170.9 0.6 gather_fusion.1
  171.5 0.9 copy.54
  (41 shorter events, 0.3 us)
Async XLA Ops:
  7.2 42.0 %copy-start = (bf16[2048,256]{1,0:T(8,128)(2,1)S(1)}, bf16[2048,256]{1,0:T(8,128)(2,1)}, u32[]{:S(2)}) copy-start(bf16[2048,256]{1,0:T(8,128)(2,1)} %param.8) | copy-start | bytes 3145732
  7.2 0.7 copy-start.12
  7.2 42.0 %all-gather.2.cloned.1.call-start = ((), (), s32[]{:S(2)}) async-start(), calls=%async_computation.2 | async-start | bytes 1179648 | tf_op jit(solution)/shard_map/all_gather | solution.py:177
  9.0 47.0 %all-to-all-start.1 = ((s32[64,1,1]{2,1,0:T(1,128)}), s32[64,1,1]{2,1,0:T(1,128)}, u32[]{:S(2)}, u32[]{:S(2)}) async-start(s32[64,1,1]{2,1,0:T(1,128)} %copy.53), calls=%async_computation.1 | async-start | bytes 65536 | tf_op jit(solution)/shard_map/all_to_all | solution.py:215
  21.8 0.7 copy-start.9
  51.1 2.6 %copy-start.2 = (bf16[256,2048]{1,0:T(8,128)(2,1)S(1)}, bf16[256,2048]{1,0:T(8,128)(2,1)}, u32[]{:S(2)}) copy-start(bf16[256,2048]{1,0:T(8,128)(2,1)} %all-gather.2.cloned.1.call-done) | copy-start | bytes 3145732
  51.2 2.6 %copy-start.3 = (bf16[2048,256]{1,0:T(8,128)(2,1)S(1)}, bf16[2048,256]{1,0:T(8,128)(2,1)}, u32[]{:S(2)}) copy-start(bf16[2048,256]{1,0:T(8,128)(2,1)} %param.9) | copy-start | bytes 3145732
  54.2 68.9 %copy-start.4 = (bf16[256,512]{1,0:T(8,128)(2,1)}, bf16[256,512]{1,0:T(8,128)(2,1)S(1)}, u32[]{:S(2)}) copy-start(bf16[256,512]{1,0:T(8,128)(2,1)S(1)} %pad_maximum_fusion.1.refs_0_.refs_5_) | copy-start | bytes 786436
  55.9 10.6 %copy-start.8 = (s32[7]{0:T(128)S(1)}, s32[7]{0:T(128)}, u32[]{:S(2)}) copy-start(s32[7]{0:T(128)} %constant.68) | copy-start | bytes 88
  55.9 22.0 %copy-start.5 = (bf16[256,2,256]{2,1,0:T(2,128)(2,1)S(1)}, bf16[256,2,256]{2,1,0:T(2,128)(2,1)}, u32[]{:S(2)}) copy-start(bf16[256,2,256]{2,1,0:T(2,128)(2,1)} %param.10) | copy-start | bytes 786436
  55.9 115.0 %all-to-all-start = ((bf16[64,16,2,256]{3,1,2,0:T(8,128)(2,1)}), bf16[64,16,2,256]{3,1,2,0:T(8,128)(2,1)S(1)}, u32[]{:S(2)}, u32[]{:S(2)}) async-start(bf16[64,16,2,256]{3,1,2,0:T(8,128)(2,1)} %gather_fusion), calls=%async_computation | async-start | bytes 2097152 | tf_op jit(solution)/shard_map/all_to_all | solution.py:214
  66.6 34.9 %collective-permute-start = (bf16[256,512]{1,0:T(8,128)(2,1)S(1)}, bf16[256,512]{1,0:T(8,128)(2,1)S(1)}, u32[]{:S(2)}, u32[]{:S(2)}) collective-permute-start(bf16[256,512]{1,0:T(8,128)(2,1)S(1)} %pad_maximum_fusion.1.refs_0_.refs_5_), channel_id=1, source_target_pairs={{0,8},{8,16},{16,24},{24,32},{32,40},{40,48},{48,56},{56,64},{64,7... | collective-permute-start | bytes 786440 | tf_op jit(solution)/shard_map/ppermute | solution.py:20
  70.0 46.3 %collective-permute-start.1 = (bf16[256,512]{1,0:T(8,128)(2,1)S(1)}, bf16[256,512]{1,0:T(8,128)(2,1)}, u32[]{:S(2)}, u32[]{:S(2)}) collective-permute-start(bf16[256,512]{1,0:T(8,128)(2,1)S(1)} %pad_maximum_fusion.1.refs_0_.refs_5_), channel_id=1, source_target_pairs={{0,24},{8,32},{16,40},{24,48},{32,56},{40,64},{48,72},{56,80},{64,... | collective-permute-start | bytes 786440 | tf_op jit(solution)/shard_map/ppermute | solution.py:20
  77.4 1.3 copy-start.7
  101.5 14.8 %copy-start.6 = (bf16[256,512]{1,0:T(8,128)(2,1)}, bf16[256,512]{1,0:T(8,128)(2,1)S(1)}, u32[]{:S(2)}) copy-start(bf16[256,512]{1,0:T(8,128)(2,1)S(1)} %collective-permute-done.refs_1_.refs_6_) | copy-start | bytes 786436
  117.3 46.0 %collective-permute-start.4 = (bf16[256,1024]{1,0:T(8,128)(2,1)S(1)}, bf16[256,1024]{1,0:T(8,128)(2,1)S(1)}, u32[]{:S(2)}, u32[]{:S(2)}) collective-permute-start(bf16[256,1024]{1,0:T(8,128)(2,1)S(1)} %pad_maximum_fusion), channel_id=1, source_target_pairs={{0,8},{8,16},{16,24},{24,32},{32,40},{40,48},{48,56},{56,64},{64,7... | collective-permute-start | bytes 1572872 | tf_op jit(solution)/shard_map/ppermute | solution.py:20
  120.1 23.7 %collective-permute-start.2 = (bf16[256,512]{1,0:T(8,128)(2,1)S(1)}, bf16[256,512]{1,0:T(8,128)(2,1)S(1)}, u32[]{:S(2)}, u32[]{:S(2)}) collective-permute-start(bf16[256,512]{1,0:T(8,128)(2,1)S(1)} %pad_maximum_fusion.1.refs_0_.refs_5_), channel_id=1, source_target_pairs={{0,40},{8,48},{16,56},{24,64},{32,72},{40,80},{48,88},{56,96},{64,... | collective-permute-start | bytes 786440 | tf_op jit(solution)/shard_map/ppermute | solution.py:20
  123.1 33.9 %collective-permute-start.3 = (bf16[256,512]{1,0:T(8,128)(2,1)S(1)}, bf16[256,512]{1,0:T(8,128)(2,1)S(1)}, u32[]{:S(2)}, u32[]{:S(2)}) collective-permute-start(bf16[256,512]{1,0:T(8,128)(2,1)S(1)} %pad_maximum_fusion.1.refs_0_.refs_5_), channel_id=1, source_target_pairs={{0,48},{8,56},{16,64},{24,72},{32,80},{40,88},{48,96},{56,104},{64... | collective-permute-start | bytes 786440 | tf_op jit(solution)/shard_map/ppermute | solution.py:20
  143.8 13.3 %copy-start.10 = (bf16[256,512]{1,0:T(8,128)(2,1)}, bf16[256,512]{1,0:T(8,128)(2,1)S(1)}, u32[]{:S(2)}) copy-start(bf16[256,512]{1,0:T(8,128)(2,1)S(1)} %collective-permute-done.2.refs_3_.refs_8_) | copy-start | bytes 786436
  157.0 0.7 copy-start.11
  163.3 0.8 copy-start.1
Sparse Core Ops, SparseCore 0:
  10.1 39.0 all-gather.1

commit v4 on v3

--- a/solution.py
+++ b/solution.py
@@ -5,6 +5,7 @@
 import jax.numpy as jnp
 from jax import lax
 from jax.experimental import pallas as pl
+from jax.experimental.pallas import tpu as pltpu
 from jax.sharding import PartitionSpec as P
 
 
@@ -28,15 +29,41 @@
     return (segment, positions - start)
 
 
-def rotate_heads(raw, offsets):
+def project_kernel(piece_ref, key_weight_ref, value_weight_ref, cosine_ref, sine_ref, out_ref):
+    piece = piece_ref[...]
+    width = key_weight_ref.shape[1]
+    keys = jnp.dot(piece, key_weight_ref[...], preferred_element_type=jnp.float32)
+    values = jnp.dot(piece, value_weight_ref[...], preferred_element_type=jnp.float32)
+    cosine = cosine_ref[...]
+    sine = sine_ref[...]
+    for head in range(width // HD):
+        raw = keys[:, head * HD : (head + 1) * HD]
+        turned = raw * cosine + pltpu.roll(raw, HD // 2, 1) * sine
+        out_ref[:, head * HD : (head + 1) * HD] = turned.astype(out_ref.dtype)
+    out_ref[:, width:] = values.astype(out_ref.dtype)
+
+
+def project(piece, key_weight, value_weight, offsets):
+    rows = piece.shape[0]
+    width = key_weight.shape[1]
     half = HD // 2
     inverse = 10000.0 ** (-(2.0 * jnp.arange(half, dtype=jnp.float32)) / HD)
     angle = offsets.astype(jnp.float32)[:, None] * inverse[None, :]
-    cosine = jnp.cos(angle)[:, None, :]
-    sine = jnp.sin(angle)[:, None, :]
-    lower = raw[..., :half]
-    upper = raw[..., half:]
-    return jnp.concatenate([lower * cosine - upper * sine, upper * cosine + lower * sine], axis=-1)
+    cosine = jnp.cos(angle)
+    sine = jnp.sin(angle)
+    cosine = jnp.concatenate([cosine, cosine], axis=1)
+    sine = jnp.concatenate([-sine, sine], axis=1)
+    cost = pl.CostEstimate(
+        flops=2 * 2 * rows * piece.shape[1] * width,
+        transcendentals=0,
+        bytes_accessed=piece.size * 2 + 2 * key_weight.size * 2 + rows * 2 * width * 2,
+    )
+    return pl.pallas_call(
+        project_kernel,
+        out_shape=jax.ShapeDtypeStruct((rows, 2 * width), jnp.bfloat16),
+        cost_estimate=cost,
+        name="project_rotate",
+    )(piece, key_weight, value_weight, cosine, sine)
 
 
 def masked_scores(query, query_segment, key_segment_ref, key_ref, slot, diagonal, scale):
@@ -175,11 +202,7 @@
     positions = first_row + jnp.arange(block_rows, dtype=jnp.int32)
     segment, offsets = segment_info(positions, prompt_pages)
     piece = lax.all_gather(tokens, "tp", axis=1, tiled=True)
-    raw_keys = jnp.dot(piece, key_weight, preferred_element_type=jnp.float32)
-    raw_values = jnp.dot(piece, value_weight, preferred_element_type=jnp.float32)
-    keys = rotate_heads(raw_keys.reshape(block_rows, local_heads, HD), offsets).astype(jnp.bfloat16)
-    values = raw_values.astype(jnp.bfloat16)
-    key_value = jnp.concatenate([keys.reshape(block_rows, width), values], axis=1)
+    key_value = project(piece, key_weight, value_weight, offsets)
     direct = (1, 3, 5, 6)
     sent = {distance: from_behind(key_value, "seq", distance) for distance in direct}
     relayed = [distance for distance in range(2, BACK + 1) if distance not in direct]

time: 180 us -> 179 us (level)
  Pallas kernels: 10.6 us -> 14 us
  other arithmetic: 6.84 us -> 3.58 us
  matrix products: 2.19 us -> 0 us
    pallas_call x0 -> x1, Pallas kernels: none -> 3.38 us  [project(): pl.pallas_call(project_kernel, out_shape=jax.ShapeDtypeStruct((rows, 2 *...]
    dot_general x2 -> x0, matrix products: 2.19 us -> none  [the longest x1 1.75 us: body(): raw_keys = jnp.dot(piece, key_weight, preferred_element_type=jnp.float32)]
    unnamed x31 -> x24, local copies, waits for them, and re-layouts: 4.89 us -> 4.5 us
  transfers between devices with their start and end apart: 8 -> 8, of which waited for: 5 -> 5; matrix products, arithmetic and copies ran while one was open for 9% -> 6% of each run, Pallas kernels for 6% -> 8%
where the time goes in v4:
time: 179 us; the launch traced here: 178 us
  waiting for transfers between devices  93 us (52%)
  starting transfers between devices  41.8 us (23%)
  between operations  14.3 us (8%)
  Pallas kernels  14 us (8%)
  local copies, waits for them, and re-layouts  11.6 us (6%)
  other arithmetic  3.58 us (2%)
    ppermute x5, waiting for transfers between devices, from_behind(): return lax.ppermute(value, axis, pairs)  67.1 us
    all_gather x1, waiting for transfers between devices, body(): piece = lax.all_gather(tokens, 'tp', axis=1, tiled=True)  25.2 us
    ppermute x5, starting transfers between devices, from_behind(): return lax.ppermute(value, axis, pairs)  18.6 us
    all_to_all x1, starting transfers between devices, body(): lax.all_to_all(labels, 'seq', split_axis=0, concat_axis=0, tiled=True)  12.6 us
    all_to_all x1, starting transfers between devices, body(): lax.all_to_all(outgoing, 'seq', split_axis=0, concat_axis=0, tiled=True)  10.6 us
    pallas_call x1, Pallas kernels, attend(): pl.pallas_call(functools.partial(first_kernel, blocks=len(first), scale=s...  5.52 us
    pallas_call x1, Pallas kernels, attend(): pl.pallas_call(functools.partial(second_kernel, blocks=len(second), scale...  5.06 us
    unnamed x24, local copies, waits for them, and re-layouts  4.5 us
  transfers between devices with their start and end apart: 8, of which 5 were waited for; matrix products, arithmetic and copies ran while one was open for 6% of the time, Pallas kernels for 8%

profile of v4, /device:TPU:6, one launch (start us, length us, event | category | flops | bytes accessed | tf_op | source)
XLA Modules:
  0.0 178.2 jit_solution(12649975223415506069)
XLA Ops:
  7.2 0.0 all-gather.2.cloned.1.call-start
  7.2 0.7 all-gather.2.cloned.1.call-update
  7.9 0.2 convert_reduce_fusion.1
  8.1 0.1 select_reduce_fusion.1
  8.2 0.7 copy.35
  8.9 12.6 %all-to-all-start.1 = ((s32[64,1,1]{2,1,0:T(1,128)}), s32[64,1,1]{2,1,0:T(1,128)S(1)}, u32[]{:S(2)}, u32[]{:S(2)}) async-start(s32[64,1,1]{2,1,0:T(1,128)} %copy.35), calls=%async_computation.1 | async-start | bytes 65536 | tf_op jit(solution)/shard_map/all_to_all | solution.py:238
  21.6 0.0 copy-start.7
  21.6 0.6 copy-done.7
  22.2 0.1 copy.31
  22.4 0.1 multiply_reduce_fusion
  22.5 0.1 fusion.2
  22.6 0.5 fusion
  23.1 0.8 pad_maximum_fusion.1
  24.0 25.2 %all-gather.2.cloned.1.call-done.piece_ref = bf16[256,2048]{1,0:T(8,128)(2,1)} async-done(((bf16[256,256]{1,0:T(8,128)(2,1)}), bf16[256,2048]{1,0:T(8,128)(2,1)}) %all-gather.2.cloned.1.call-update) | async-done | bytes 1048592 | tf_op jit(solution)/shard_map/all_gather | solution.py:204
  49.2 3.4 %project_rotate.1.refs_0_.refs_5_ = bf16[256,512]{1,0:T(8,128)(2,1)} custom-call(bf16[256,2048]{1,0:T(8,128)(2,1)} %all-gather.2.cloned.1.call-done.piece_ref, bf16[2048,256]{1,0:T(8,128)(2,1)} %key_weight_ref.1, bf16[2048,256]{1,0:T(8,128)(2,1)} %value_weight_ref.1, f32[256,128]{1,0:T(8,128)} %get-tuple-element.27.cosine_ref, ...), custom_call_target="tpu_custom_call" | custom-call | flops 536870912 | bytes 3407872 | tf_op jit(solution)/shard_map/project_rotate/pallas_call | solution.py:61
  52.6 1.0 reshape.264
  53.6 1.6 gather_fusion
  55.2 0.0 all-to-all-done.1
  55.2 10.6 %all-to-all-start = ((bf16[64,16,2,256]{3,1,2,0:T(8,128)(2,1)}), bf16[64,16,2,256]{3,1,2,0:T(8,128)(2,1)S(1)}, u32[]{:S(2)}, u32[]{:S(2)}) async-start(bf16[64,16,2,256]{3,1,2,0:T(8,128)(2,1)} %gather_fusion), calls=%async_computation | async-start | bytes 2097152 | tf_op jit(solution)/shard_map/all_to_all | solution.py:237
  65.9 0.1 broadcast_add_fusion
  65.9 3.4 %collective-permute-start = (bf16[256,512]{1,0:T(8,128)(2,1)S(1)}, bf16[256,512]{1,0:T(8,128)(2,1)S(1)}, u32[]{:S(2)}, u32[]{:S(2)}) collective-permute-start(bf16[256,512]{1,0:T(8,128)(2,1)S(1)} %copy-done.1), channel_id=1, source_target_pairs={{0,8},{8,16},{16,24},{24,32},{32,40},{40,48},{48,56},{56,64},{64,7... | collective-permute-start | bytes 786440 | tf_op jit(solution)/shard_map/ppermute | solution.py:21
  69.3 6.4 %collective-permute-start.1 = (bf16[256,512]{1,0:T(8,128)(2,1)S(1)}, bf16[256,512]{1,0:T(8,128)(2,1)S(1)}, u32[]{:S(2)}, u32[]{:S(2)}) collective-permute-start(bf16[256,512]{1,0:T(8,128)(2,1)S(1)} %copy-done.1), channel_id=1, source_target_pairs={{0,24},{8,32},{16,40},{24,48},{32,56},{40,64},{48,72},{56,80},{64,... | collective-permute-start | bytes 786440 | tf_op jit(solution)/shard_map/ppermute | solution.py:21
  75.7 0.1 convert_reduce_fusion
  75.8 0.8 copy.33.query_segment_ref
  76.6 0.1 compare_select_fusion.1
  76.7 0.6 slice.12.key_segment_ref
  77.3 0.7 copy.37
  78.0 1.2 reduce.3
  79.2 21.6 %collective-permute-done.refs_1_.refs_6_ = bf16[256,512]{1,0:T(8,128)(2,1)S(1)} collective-permute-done((bf16[256,512]{1,0:T(8,128)(2,1)S(1)}, bf16[256,512]{1,0:T(8,128)(2,1)S(1)}, u32[]{:S(2)}, u32[]{:S(2)}) %collective-permute-start) | collective-permute-done | bytes 262176 | tf_op jit(solution)/shard_map/ppermute | solution.py:21
  100.8 14.7 %collective-permute-done.1.refs_2_.refs_7_ = bf16[256,512]{1,0:T(8,128)(2,1)S(1)} collective-permute-done((bf16[256,512]{1,0:T(8,128)(2,1)S(1)}, bf16[256,512]{1,0:T(8,128)(2,1)S(1)}, u32[]{:S(2)}, u32[]{:S(2)}) %collective-permute-start.1) | collective-permute-done | bytes 262176 | tf_op jit(solution)/shard_map/ppermute | solution.py:21
  115.5 0.1 pad_maximum_fusion
  115.6 0.6 copy-done.4
  116.2 2.7 %collective-permute-start.4 = (bf16[256,1024]{1,0:T(8,128)(2,1)S(1)}, bf16[256,1024]{1,0:T(8,128)(2,1)S(1)}, u32[]{:S(2)}, u32[]{:S(2)}) collective-permute-start(bf16[256,1024]{1,0:T(8,128)(2,1)S(1)} %pad_maximum_fusion), channel_id=1, source_target_pairs={{0,8},{8,16},{16,24},{24,32},{32,40},{40,48},{48,56},{56,64},{64,7... | collective-permute-start | bytes 1572872 | tf_op jit(solution)/shard_map/ppermute | solution.py:21
  118.9 0.1 select_reduce_fusion
  119.0 3.0 %collective-permute-start.2 = (bf16[256,512]{1,0:T(8,128)(2,1)S(1)}, bf16[256,512]{1,0:T(8,128)(2,1)S(1)}, u32[]{:S(2)}, u32[]{:S(2)}) collective-permute-start(bf16[256,512]{1,0:T(8,128)(2,1)S(1)} %copy-done.1), channel_id=1, source_target_pairs={{0,40},{8,48},{16,56},{24,64},{32,72},{40,80},{48,88},{56,96},{64,... | collective-permute-start | bytes 786440 | tf_op jit(solution)/shard_map/ppermute | solution.py:21
  122.0 3.1 %collective-permute-start.3 = (bf16[256,512]{1,0:T(8,128)(2,1)S(1)}, bf16[256,512]{1,0:T(8,128)(2,1)S(1)}, u32[]{:S(2)}, u32[]{:S(2)}) collective-permute-start(bf16[256,512]{1,0:T(8,128)(2,1)S(1)} %copy-done.1), channel_id=1, source_target_pairs={{0,48},{8,56},{16,64},{24,72},{32,80},{40,88},{48,96},{56,104},{64... | collective-permute-start | bytes 786440 | tf_op jit(solution)/shard_map/ppermute | solution.py:21
  125.2 17.5 %collective-permute-done.2.refs_3_.refs_8_ = bf16[256,512]{1,0:T(8,128)(2,1)S(1)} collective-permute-done((bf16[256,512]{1,0:T(8,128)(2,1)S(1)}, bf16[256,512]{1,0:T(8,128)(2,1)S(1)}, u32[]{:S(2)}, u32[]{:S(2)}) %collective-permute-start.2) | collective-permute-done | bytes 262176 | tf_op jit(solution)/shard_map/ppermute | solution.py:21
  142.6 13.3 %collective-permute-done.3.refs_4_.refs_9_ = bf16[256,512]{1,0:T(8,128)(2,1)S(1)} collective-permute-done((bf16[256,512]{1,0:T(8,128)(2,1)S(1)}, bf16[256,512]{1,0:T(8,128)(2,1)S(1)}, u32[]{:S(2)}, u32[]{:S(2)}) %collective-permute-start.3) | collective-permute-done | bytes 262176 | tf_op jit(solution)/shard_map/ppermute | solution.py:21
  156.0 0.0 copy-done.8
  156.0 0.7 copy-done.9
  156.7 5.5 %first_blocks.1 = (f32[256,512]{1,0:T(8,128)}, f32[256,512]{1,0:T(8,128)}, f32[256,512]{1,0:T(8,128)}) custom-call(s32[256,1]{1,0:T(8,128)} %copy.33.query_segment_ref, s32[5,256]{1,0:T(8,128)} %bitcast.18, bf16[256,512]{1,0:T(8,128)(2,1)} %bitcast.15, bf16[256,512]{1,0:T(8,128)(2,1)} %project_rotate.1.refs_0_.refs_5_, bf16[256,512]{1,0:T(8,128)(2,1)} %copy-done.3, ...), custom_call_target="tpu_custom_call" | custom-call | flops 1006632960 | bytes 3145728 | tf_op jit(solution)/shard_map/first_blocks/pallas_call | solution.py:175
  162.2 0.0 collective-permute-done.4.refs_0_.refs_1_.refs_2_.refs_3_
  162.2 0.8 copy-done
  163.0 5.1 %second_blocks.1 = bf16[256,512]{1,0:T(8,128)(2,1)} custom-call(s32[256,1]{1,0:T(8,128)} %copy.33.query_segment_ref, s32[2,256]{1,0:T(2,128)} %slice.12.key_segment_ref, bf16[256,512]{1,0:T(8,128)(2,1)} %bitcast.16, f32[256,512]{1,0:T(8,128)} %get-tuple-element.5.peak_ref, f32[256,512]{1,0:T(8,128)} %get-tuple-element.6.total_ref, ...), custom_call_target="tpu_custom_call" | custom-call | flops 402653184 | bytes 2359296 | tf_op jit(solution)/shard_map/second_blocks/pallas_call | solution.py:185
  168.1 1.7 reshape.263
  169.8 0.0 all-to-all-done
  169.8 0.6 gather_fusion.1
  170.4 0.9 copy.36
  (30 shorter events, 0.2 us)
Async XLA Ops:
  7.2 0.7 copy-start.10
  7.2 42.0 %all-gather.2.cloned.1.call-start = ((), (), s32[]{:S(2)}) async-start(), calls=%async_computation.2 | async-start | bytes 1179648 | tf_op jit(solution)/shard_map/all_gather | solution.py:204
  8.9 46.3 %all-to-all-start.1 = ((s32[64,1,1]{2,1,0:T(1,128)}), s32[64,1,1]{2,1,0:T(1,128)S(1)}, u32[]{:S(2)}, u32[]{:S(2)}) async-start(s32[64,1,1]{2,1,0:T(1,128)} %copy.35), calls=%async_computation.1 | async-start | bytes 65536 | tf_op jit(solution)/shard_map/all_to_all | solution.py:238
  21.6 0.7 copy-start.7
  55.2 10.6 %copy-start.6 = (s32[7]{0:T(128)S(1)}, s32[7]{0:T(128)}, u32[]{:S(2)}) copy-start(s32[7]{0:T(128)} %constant.68) | copy-start | bytes 88
  55.2 10.7 %copy-start.1 = (bf16[256,512]{1,0:T(8,128)(2,1)S(1)}, bf16[256,512]{1,0:T(8,128)(2,1)}, u32[]{:S(2)}) copy-start(bf16[256,512]{1,0:T(8,128)(2,1)} %project_rotate.1.refs_0_.refs_5_) | copy-start | bytes 786436
  55.2 22.0 %copy-start.2 = (bf16[256,2,256]{2,1,0:T(2,128)(2,1)S(1)}, bf16[256,2,256]{2,1,0:T(2,128)(2,1)}, u32[]{:S(2)}) copy-start(bf16[256,2,256]{2,1,0:T(2,128)(2,1)} %param.10) | copy-start | bytes 786436
  55.2 114.6 %all-to-all-start = ((bf16[64,16,2,256]{3,1,2,0:T(8,128)(2,1)}), bf16[64,16,2,256]{3,1,2,0:T(8,128)(2,1)S(1)}, u32[]{:S(2)}, u32[]{:S(2)}) async-start(bf16[64,16,2,256]{3,1,2,0:T(8,128)(2,1)} %gather_fusion), calls=%async_computation | async-start | bytes 2097152 | tf_op jit(solution)/shard_map/all_to_all | solution.py:237
  65.9 34.9 %collective-permute-start = (bf16[256,512]{1,0:T(8,128)(2,1)S(1)}, bf16[256,512]{1,0:T(8,128)(2,1)S(1)}, u32[]{:S(2)}, u32[]{:S(2)}) collective-permute-start(bf16[256,512]{1,0:T(8,128)(2,1)S(1)} %copy-done.1), channel_id=1, source_target_pairs={{0,8},{8,16},{16,24},{24,32},{32,40},{40,48},{48,56},{56,64},{64,7... | collective-permute-start | bytes 786440 | tf_op jit(solution)/shard_map/ppermute | solution.py:21
  69.3 46.2 %collective-permute-start.1 = (bf16[256,512]{1,0:T(8,128)(2,1)S(1)}, bf16[256,512]{1,0:T(8,128)(2,1)S(1)}, u32[]{:S(2)}, u32[]{:S(2)}) collective-permute-start(bf16[256,512]{1,0:T(8,128)(2,1)S(1)} %copy-done.1), channel_id=1, source_target_pairs={{0,24},{8,32},{16,40},{24,48},{32,56},{40,64},{48,72},{56,80},{64,... | collective-permute-start | bytes 786440 | tf_op jit(solution)/shard_map/ppermute | solution.py:21
  76.7 1.3 copy-start.5
  100.8 14.7 %copy-start.3 = (bf16[256,512]{1,0:T(8,128)(2,1)}, bf16[256,512]{1,0:T(8,128)(2,1)S(1)}, u32[]{:S(2)}) copy-start(bf16[256,512]{1,0:T(8,128)(2,1)S(1)} %collective-permute-done.refs_1_.refs_6_) | copy-start | bytes 786436
  115.5 0.7 copy-start.4
  116.2 46.0 %collective-permute-start.4 = (bf16[256,1024]{1,0:T(8,128)(2,1)S(1)}, bf16[256,1024]{1,0:T(8,128)(2,1)S(1)}, u32[]{:S(2)}, u32[]{:S(2)}) collective-permute-start(bf16[256,1024]{1,0:T(8,128)(2,1)S(1)} %pad_maximum_fusion), channel_id=1, source_target_pairs={{0,8},{8,16},{16,24},{24,32},{32,40},{40,48},{48,56},{56,64},{64,7... | collective-permute-start | bytes 1572872 | tf_op jit(solution)/shard_map/ppermute | solution.py:21
  119.0 23.6 %collective-permute-start.2 = (bf16[256,512]{1,0:T(8,128)(2,1)S(1)}, bf16[256,512]{1,0:T(8,128)(2,1)S(1)}, u32[]{:S(2)}, u32[]{:S(2)}) collective-permute-start(bf16[256,512]{1,0:T(8,128)(2,1)S(1)} %copy-done.1), channel_id=1, source_target_pairs={{0,40},{8,48},{16,56},{24,64},{32,72},{40,80},{48,88},{56,96},{64,... | collective-permute-start | bytes 786440 | tf_op jit(solution)/shard_map/ppermute | solution.py:21
  122.0 33.9 %collective-permute-start.3 = (bf16[256,512]{1,0:T(8,128)(2,1)S(1)}, bf16[256,512]{1,0:T(8,128)(2,1)S(1)}, u32[]{:S(2)}, u32[]{:S(2)}) collective-permute-start(bf16[256,512]{1,0:T(8,128)(2,1)S(1)} %copy-done.1), channel_id=1, source_target_pairs={{0,48},{8,56},{16,64},{24,72},{32,80},{40,88},{48,96},{56,104},{64... | collective-permute-start | bytes 786440 | tf_op jit(solution)/shard_map/ppermute | solution.py:21
  142.6 13.3 %copy-start.8 = (bf16[256,512]{1,0:T(8,128)(2,1)}, bf16[256,512]{1,0:T(8,128)(2,1)S(1)}, u32[]{:S(2)}) copy-start(bf16[256,512]{1,0:T(8,128)(2,1)S(1)} %collective-permute-done.2.refs_3_.refs_8_) | copy-start | bytes 786436
  156.0 0.7 copy-start.9
  162.2 0.8 copy-start
Sparse Core Ops, SparseCore 0:
  10.1 39.0 all-gather.1

commit v5 on v4

--- a/solution.py
+++ b/solution.py
@@ -30,10 +30,21 @@
 
 
 def project_kernel(piece_ref, key_weight_ref, value_weight_ref, cosine_ref, sine_ref, out_ref):
-    piece = piece_ref[...]
+    rows = out_ref.shape[0]
     width = key_weight_ref.shape[1]
-    keys = jnp.dot(piece, key_weight_ref[...], preferred_element_type=jnp.float32)
-    values = jnp.dot(piece, value_weight_ref[...], preferred_element_type=jnp.float32)
+    share = piece_ref.shape[1]
+    keys = jnp.zeros((rows, width), jnp.float32)
+    values = jnp.zeros((rows, width), jnp.float32)
+    for part in range(piece_ref.shape[0] // rows):
+        chunk = piece_ref[part * rows : (part + 1) * rows, :]
+        keys = keys + jnp.dot(
+            chunk, key_weight_ref[part * share : (part + 1) * share, :],
+            preferred_element_type=jnp.float32,
+        )
+        values = values + jnp.dot(
+            chunk, value_weight_ref[part * share : (part + 1) * share, :],
+            preferred_element_type=jnp.float32,
+        )
     cosine = cosine_ref[...]
     sine = sine_ref[...]
     for head in range(width // HD):
@@ -44,7 +55,7 @@
 
 
 def project(piece, key_weight, value_weight, offsets):
-    rows = piece.shape[0]
+    rows = offsets.shape[0]
     width = key_weight.shape[1]
     half = HD // 2
     inverse = 10000.0 ** (-(2.0 * jnp.arange(half, dtype=jnp.float32)) / HD)
@@ -54,7 +65,7 @@
     cosine = jnp.concatenate([cosine, cosine], axis=1)
     sine = jnp.concatenate([-sine, sine], axis=1)
     cost = pl.CostEstimate(
-        flops=2 * 2 * rows * piece.shape[1] * width,
+        flops=2 * 2 * rows * key_weight.shape[0] * width,
         transcendentals=0,
         bytes_accessed=piece.size * 2 + 2 * key_weight.size * 2 + rows * 2 * width * 2,
     )
@@ -201,7 +212,7 @@
     first_row = lax.axis_index("seq") * block_rows
     positions = first_row + jnp.arange(block_rows, dtype=jnp.int32)
     segment, offsets = segment_info(positions, prompt_pages)
-    piece = lax.all_gather(tokens, "tp", axis=1, tiled=True)
+    piece = lax.all_gather(tokens, "tp", axis=0, tiled=True)
     key_value = project(piece, key_weight, value_weight, offsets)
     direct = (1, 3, 5, 6)
     sent = {distance: from_behind(key_value, "seq", distance) for distance in direct}

time: 179 us -> 178 us (level)
  no operation moved by 1% of the time
where the time goes in v5:
time: 178 us; the launch traced here: 177 us
  waiting for transfers between devices  92 us (52%)
  starting transfers between devices  41.8 us (23%)
  between operations  14.3 us (8%)
  Pallas kernels  14 us (8%)
  local copies, waits for them, and re-layouts  11.6 us (7%)
  other arithmetic  3.58 us (2%)
    ppermute x5, waiting for transfers between devices, from_behind(): return lax.ppermute(value, axis, pairs)  67 us
    all_gather x1, waiting for transfers between devices, body(): piece = lax.all_gather(tokens, 'tp', axis=0, tiled=True)  24.2 us
    ppermute x5, starting transfers between devices, from_behind(): return lax.ppermute(value, axis, pairs)  18.6 us
    all_to_all x1, starting transfers between devices, body(): lax.all_to_all(labels, 'seq', split_axis=0, concat_axis=0, tiled=True)  12.6 us
    all_to_all x1, starting transfers between devices, body(): lax.all_to_all(outgoing, 'seq', split_axis=0, concat_axis=0, tiled=True)  10.6 us
    pallas_call x1, Pallas kernels, attend(): pl.pallas_call(functools.partial(first_kernel, blocks=len(first), scale=s...  5.54 us
    pallas_call x1, Pallas kernels, attend(): pl.pallas_call(functools.partial(second_kernel, blocks=len(second), scale...  5.06 us
    unnamed x24, local copies, waits for them, and re-layouts  4.5 us
  transfers between devices with their start and end apart: 8, of which 5 were waited for; matrix products, arithmetic and copies ran while one was open for 6% of the time, Pallas kernels for 8%

profile of v5, /device:TPU:6, one launch (start us, length us, event | category | flops | bytes accessed | tf_op | source)
XLA Modules:
  0.0 177.2 jit_solution(18232405963662356652)
XLA Ops:
  7.2 0.0 all-gather.2.cloned.1.call-start
  7.2 0.7 all-gather.2.cloned.1.call-update
  7.9 0.2 convert_reduce_fusion.1
  8.1 0.1 select_reduce_fusion.1
  8.2 0.7 copy.35
  8.9 12.6 %all-to-all-start.1 = ((s32[64,1,1]{2,1,0:T(1,128)}), s32[64,1,1]{2,1,0:T(1,128)S(1)}, u32[]{:S(2)}, u32[]{:S(2)}) async-start(s32[64,1,1]{2,1,0:T(1,128)} %copy.35), calls=%async_computation.1 | async-start | bytes 65536 | tf_op jit(solution)/shard_map/all_to_all | solution.py:249
  21.6 0.0 copy-start.7
  21.6 0.6 copy-done.7
  22.2 0.1 copy.31
  22.4 0.1 multiply_reduce_fusion
  22.5 0.1 fusion.2
  22.6 0.5 fusion
  23.1 0.8 pad_maximum_fusion.1
  24.0 24.2 %all-gather.2.cloned.1.call-done.piece_ref = bf16[2048,256]{1,0:T(8,128)(2,1)} async-done(((bf16[256,256]{1,0:T(8,128)(2,1)}), bf16[2048,256]{1,0:T(8,128)(2,1)}) %all-gather.2.cloned.1.call-update) | async-done | bytes 1048592 | tf_op jit(solution)/shard_map/all_gather | solution.py:215
  48.2 3.4 %project_rotate.1.refs_0_.refs_5_ = bf16[256,512]{1,0:T(8,128)(2,1)} custom-call(bf16[2048,256]{1,0:T(8,128)(2,1)} %all-gather.2.cloned.1.call-done.piece_ref, bf16[2048,256]{1,0:T(8,128)(2,1)} %key_weight_ref.1, bf16[2048,256]{1,0:T(8,128)(2,1)} %value_weight_ref.1, f32[256,128]{1,0:T(8,128)} %get-tuple-element.27.cosine_ref, ...), custom_call_target="tpu_custom_call" | custom-call | flops 536870912 | bytes 3407872 | tf_op jit(solution)/shard_map/project_rotate/pallas_call | solution.py:72
  51.6 1.0 reshape.264
  52.6 1.6 gather_fusion
  54.2 0.0 all-to-all-done.1
  54.2 10.6 %all-to-all-start = ((bf16[64,16,2,256]{3,1,2,0:T(8,128)(2,1)}), bf16[64,16,2,256]{3,1,2,0:T(8,128)(2,1)S(1)}, u32[]{:S(2)}, u32[]{:S(2)}) async-start(bf16[64,16,2,256]{3,1,2,0:T(8,128)(2,1)} %gather_fusion), calls=%async_computation | async-start | bytes 2097152 | tf_op jit(solution)/shard_map/all_to_all | solution.py:248
  64.8 0.0 copy-done.6
  64.9 0.1 broadcast_add_fusion
  64.9 3.4 %collective-permute-start = (bf16[256,512]{1,0:T(8,128)(2,1)S(1)}, bf16[256,512]{1,0:T(8,128)(2,1)S(1)}, u32[]{:S(2)}, u32[]{:S(2)}) collective-permute-start(bf16[256,512]{1,0:T(8,128)(2,1)S(1)} %copy-done.1), channel_id=1, source_target_pairs={{0,8},{8,16},{16,24},{24,32},{32,40},{40,48},{48,56},{56,64},{64,7... | collective-permute-start | bytes 786440 | tf_op jit(solution)/shard_map/ppermute | solution.py:21
  68.3 6.4 %collective-permute-start.1 = (bf16[256,512]{1,0:T(8,128)(2,1)S(1)}, bf16[256,512]{1,0:T(8,128)(2,1)S(1)}, u32[]{:S(2)}, u32[]{:S(2)}) collective-permute-start(bf16[256,512]{1,0:T(8,128)(2,1)S(1)} %copy-done.1), channel_id=1, source_target_pairs={{0,24},{8,32},{16,40},{24,48},{32,56},{40,64},{48,72},{56,80},{64,... | collective-permute-start | bytes 786440 | tf_op jit(solution)/shard_map/ppermute | solution.py:21
  74.7 0.1 convert_reduce_fusion
  74.8 0.8 copy.33.query_segment_ref
  75.6 0.1 compare_select_fusion.1
  75.7 0.6 slice.12.key_segment_ref
  76.3 0.7 copy.37
  77.0 1.2 reduce.3
  78.2 21.6 %collective-permute-done.refs_1_.refs_6_ = bf16[256,512]{1,0:T(8,128)(2,1)S(1)} collective-permute-done((bf16[256,512]{1,0:T(8,128)(2,1)S(1)}, bf16[256,512]{1,0:T(8,128)(2,1)S(1)}, u32[]{:S(2)}, u32[]{:S(2)}) %collective-permute-start) | collective-permute-done | bytes 262176 | tf_op jit(solution)/shard_map/ppermute | solution.py:21
  99.8 14.7 %collective-permute-done.1.refs_2_.refs_7_ = bf16[256,512]{1,0:T(8,128)(2,1)S(1)} collective-permute-done((bf16[256,512]{1,0:T(8,128)(2,1)S(1)}, bf16[256,512]{1,0:T(8,128)(2,1)S(1)}, u32[]{:S(2)}, u32[]{:S(2)}) %collective-permute-start.1) | collective-permute-done | bytes 262176 | tf_op jit(solution)/shard_map/ppermute | solution.py:21
  114.5 0.1 pad_maximum_fusion
  114.6 0.6 copy-done.4
  115.2 2.7 %collective-permute-start.4 = (bf16[256,1024]{1,0:T(8,128)(2,1)S(1)}, bf16[256,1024]{1,0:T(8,128)(2,1)S(1)}, u32[]{:S(2)}, u32[]{:S(2)}) collective-permute-start(bf16[256,1024]{1,0:T(8,128)(2,1)S(1)} %pad_maximum_fusion), channel_id=1, source_target_pairs={{0,8},{8,16},{16,24},{24,32},{32,40},{40,48},{48,56},{56,64},{64,7... | collective-permute-start | bytes 1572872 | tf_op jit(solution)/shard_map/ppermute | solution.py:21
  117.9 0.1 select_reduce_fusion
  118.0 3.0 %collective-permute-start.2 = (bf16[256,512]{1,0:T(8,128)(2,1)S(1)}, bf16[256,512]{1,0:T(8,128)(2,1)S(1)}, u32[]{:S(2)}, u32[]{:S(2)}) collective-permute-start(bf16[256,512]{1,0:T(8,128)(2,1)S(1)} %copy-done.1), channel_id=1, source_target_pairs={{0,40},{8,48},{16,56},{24,64},{32,72},{40,80},{48,88},{56,96},{64,... | collective-permute-start | bytes 786440 | tf_op jit(solution)/shard_map/ppermute | solution.py:21
  121.0 3.1 %collective-permute-start.3 = (bf16[256,512]{1,0:T(8,128)(2,1)S(1)}, bf16[256,512]{1,0:T(8,128)(2,1)S(1)}, u32[]{:S(2)}, u32[]{:S(2)}) collective-permute-start(bf16[256,512]{1,0:T(8,128)(2,1)S(1)} %copy-done.1), channel_id=1, source_target_pairs={{0,48},{8,56},{16,64},{24,72},{32,80},{40,88},{48,96},{56,104},{64... | collective-permute-start | bytes 786440 | tf_op jit(solution)/shard_map/ppermute | solution.py:21
  124.2 17.5 %collective-permute-done.2.refs_3_.refs_8_ = bf16[256,512]{1,0:T(8,128)(2,1)S(1)} collective-permute-done((bf16[256,512]{1,0:T(8,128)(2,1)S(1)}, bf16[256,512]{1,0:T(8,128)(2,1)S(1)}, u32[]{:S(2)}, u32[]{:S(2)}) %collective-permute-start.2) | collective-permute-done | bytes 262176 | tf_op jit(solution)/shard_map/ppermute | solution.py:21
  141.6 13.3 %collective-permute-done.3.refs_4_.refs_9_ = bf16[256,512]{1,0:T(8,128)(2,1)S(1)} collective-permute-done((bf16[256,512]{1,0:T(8,128)(2,1)S(1)}, bf16[256,512]{1,0:T(8,128)(2,1)S(1)}, u32[]{:S(2)}, u32[]{:S(2)}) %collective-permute-start.3) | collective-permute-done | bytes 262176 | tf_op jit(solution)/shard_map/ppermute | solution.py:21
  155.0 0.7 copy-done.9
  155.7 5.5 %first_blocks.1 = (f32[256,512]{1,0:T(8,128)}, f32[256,512]{1,0:T(8,128)}, f32[256,512]{1,0:T(8,128)}) custom-call(s32[256,1]{1,0:T(8,128)} %copy.33.query_segment_ref, s32[5,256]{1,0:T(8,128)} %bitcast.18, bf16[256,512]{1,0:T(8,128)(2,1)} %bitcast.15, bf16[256,512]{1,0:T(8,128)(2,1)} %project_rotate.1.refs_0_.refs_5_, bf16[256,512]{1,0:T(8,128)(2,1)} %copy-done.3, ...), custom_call_target="tpu_custom_call" | custom-call | flops 1006632960 | bytes 3145728 | tf_op jit(solution)/shard_map/first_blocks/pallas_call | solution.py:186
  161.2 0.0 collective-permute-done.4.refs_0_.refs_1_.refs_2_.refs_3_
  161.2 0.8 copy-done
  162.0 5.1 %second_blocks.1 = bf16[256,512]{1,0:T(8,128)(2,1)} custom-call(s32[256,1]{1,0:T(8,128)} %copy.33.query_segment_ref, s32[2,256]{1,0:T(2,128)} %slice.12.key_segment_ref, bf16[256,512]{1,0:T(8,128)(2,1)} %bitcast.16, f32[256,512]{1,0:T(8,128)} %get-tuple-element.5.peak_ref, f32[256,512]{1,0:T(8,128)} %get-tuple-element.6.total_ref, ...), custom_call_target="tpu_custom_call" | custom-call | flops 402653184 | bytes 2359296 | tf_op jit(solution)/shard_map/second_blocks/pallas_call | solution.py:196
  167.1 1.7 reshape.263
  168.8 0.0 all-to-all-done
  168.8 0.6 gather_fusion.1
  169.4 0.9 copy.36
  (30 shorter events, 0.2 us)
Async XLA Ops:
  7.2 0.7 copy-start.10
  7.2 41.0 %all-gather.2.cloned.1.call-start = ((), (), s32[]{:S(2)}) async-start(), calls=%async_computation.2 | async-start | bytes 1179648 | tf_op jit(solution)/shard_map/all_gather | solution.py:215
  8.9 45.3 %all-to-all-start.1 = ((s32[64,1,1]{2,1,0:T(1,128)}), s32[64,1,1]{2,1,0:T(1,128)S(1)}, u32[]{:S(2)}, u32[]{:S(2)}) async-start(s32[64,1,1]{2,1,0:T(1,128)} %copy.35), calls=%async_computation.1 | async-start | bytes 65536 | tf_op jit(solution)/shard_map/all_to_all | solution.py:249
  21.6 0.7 copy-start.7
  54.2 10.6 %copy-start.6 = (s32[7]{0:T(128)S(1)}, s32[7]{0:T(128)}, u32[]{:S(2)}) copy-start(s32[7]{0:T(128)} %constant.68) | copy-start | bytes 88
  54.2 10.7 %copy-start.1 = (bf16[256,512]{1,0:T(8,128)(2,1)S(1)}, bf16[256,512]{1,0:T(8,128)(2,1)}, u32[]{:S(2)}) copy-start(bf16[256,512]{1,0:T(8,128)(2,1)} %project_rotate.1.refs_0_.refs_5_) | copy-start | bytes 786436
  54.2 22.0 %copy-start.2 = (bf16[256,2,256]{2,1,0:T(2,128)(2,1)S(1)}, bf16[256,2,256]{2,1,0:T(2,128)(2,1)}, u32[]{:S(2)}) copy-start(bf16[256,2,256]{2,1,0:T(2,128)(2,1)} %param.10) | copy-start | bytes 786436
  54.2 114.6 %all-to-all-start = ((bf16[64,16,2,256]{3,1,2,0:T(8,128)(2,1)}), bf16[64,16,2,256]{3,1,2,0:T(8,128)(2,1)S(1)}, u32[]{:S(2)}, u32[]{:S(2)}) async-start(bf16[64,16,2,256]{3,1,2,0:T(8,128)(2,1)} %gather_fusion), calls=%async_computation | async-start | bytes 2097152 | tf_op jit(solution)/shard_map/all_to_all | solution.py:248
  64.9 34.9 %collective-permute-start = (bf16[256,512]{1,0:T(8,128)(2,1)S(1)}, bf16[256,512]{1,0:T(8,128)(2,1)S(1)}, u32[]{:S(2)}, u32[]{:S(2)}) collective-permute-start(bf16[256,512]{1,0:T(8,128)(2,1)S(1)} %copy-done.1), channel_id=1, source_target_pairs={{0,8},{8,16},{16,24},{24,32},{32,40},{40,48},{48,56},{56,64},{64,7... | collective-permute-start | bytes 786440 | tf_op jit(solution)/shard_map/ppermute | solution.py:21
  68.3 46.2 %collective-permute-start.1 = (bf16[256,512]{1,0:T(8,128)(2,1)S(1)}, bf16[256,512]{1,0:T(8,128)(2,1)S(1)}, u32[]{:S(2)}, u32[]{:S(2)}) collective-permute-start(bf16[256,512]{1,0:T(8,128)(2,1)S(1)} %copy-done.1), channel_id=1, source_target_pairs={{0,24},{8,32},{16,40},{24,48},{32,56},{40,64},{48,72},{56,80},{64,... | collective-permute-start | bytes 786440 | tf_op jit(solution)/shard_map/ppermute | solution.py:21
  75.7 1.3 copy-start.5
  99.8 14.7 %copy-start.3 = (bf16[256,512]{1,0:T(8,128)(2,1)}, bf16[256,512]{1,0:T(8,128)(2,1)S(1)}, u32[]{:S(2)}) copy-start(bf16[256,512]{1,0:T(8,128)(2,1)S(1)} %collective-permute-done.refs_1_.refs_6_) | copy-start | bytes 786436
  114.5 0.7 copy-start.4
  115.2 46.0 %collective-permute-start.4 = (bf16[256,1024]{1,0:T(8,128)(2,1)S(1)}, bf16[256,1024]{1,0:T(8,128)(2,1)S(1)}, u32[]{:S(2)}, u32[]{:S(2)}) collective-permute-start(bf16[256,1024]{1,0:T(8,128)(2,1)S(1)} %pad_maximum_fusion), channel_id=1, source_target_pairs={{0,8},{8,16},{16,24},{24,32},{32,40},{40,48},{48,56},{56,64},{64,7... | collective-permute-start | bytes 1572872 | tf_op jit(solution)/shard_map/ppermute | solution.py:21
  118.0 23.6 %collective-permute-start.2 = (bf16[256,512]{1,0:T(8,128)(2,1)S(1)}, bf16[256,512]{1,0:T(8,128)(2,1)S(1)}, u32[]{:S(2)}, u32[]{:S(2)}) collective-permute-start(bf16[256,512]{1,0:T(8,128)(2,1)S(1)} %copy-done.1), channel_id=1, source_target_pairs={{0,40},{8,48},{16,56},{24,64},{32,72},{40,80},{48,88},{56,96},{64,... | collective-permute-start | bytes 786440 | tf_op jit(solution)/shard_map/ppermute | solution.py:21
  121.0 33.9 %collective-permute-start.3 = (bf16[256,512]{1,0:T(8,128)(2,1)S(1)}, bf16[256,512]{1,0:T(8,128)(2,1)S(1)}, u32[]{:S(2)}, u32[]{:S(2)}) collective-permute-start(bf16[256,512]{1,0:T(8,128)(2,1)S(1)} %copy-done.1), channel_id=1, source_target_pairs={{0,48},{8,56},{16,64},{24,72},{32,80},{40,88},{48,96},{56,104},{64... | collective-permute-start | bytes 786440 | tf_op jit(solution)/shard_map/ppermute | solution.py:21
  141.6 13.3 %copy-start.8 = (bf16[256,512]{1,0:T(8,128)(2,1)}, bf16[256,512]{1,0:T(8,128)(2,1)S(1)}, u32[]{:S(2)}) copy-start(bf16[256,512]{1,0:T(8,128)(2,1)S(1)} %collective-permute-done.2.refs_3_.refs_8_) | copy-start | bytes 786436
  155.0 0.7 copy-start.9
  161.2 0.8 copy-start
Sparse Core Ops, SparseCore 0:
  10.1 38.0 all-gather.1

commit v6 on v5

--- a/solution.py
+++ b/solution.py
@@ -214,8 +214,13 @@
     segment, offsets = segment_info(positions, prompt_pages)
     piece = lax.all_gather(tokens, "tp", axis=0, tiled=True)
     key_value = project(piece, key_weight, value_weight, offsets)
-    direct = (1, 3, 5, 6)
-    sent = {distance: from_behind(key_value, "seq", distance) for distance in direct}
+    near, far = (1, 3), (5, 6)
+    direct = near + far
+    sent = {}
+    for distance in near:
+        sent[distance] = from_behind(key_value, "seq", distance)
+    for distance in far:
+        sent[distance] = from_behind(key_value, "seq", distance)
     relayed = [distance for distance in range(2, BACK + 1) if distance not in direct]
     onward = from_behind(
         jnp.concatenate([sent[distance - 1] for distance in relayed], axis=1), "seq", 1

time: 178 us -> 178 us (level)
  no operation moved by 1% of the time
where the time goes in v6:
time: 178 us; the launch traced here: 177 us
  waiting for transfers between devices  92 us (52%)
  starting transfers between devices  41.8 us (23%)
  between operations  14.3 us (8%)
  Pallas kernels  14 us (8%)
  local copies, waits for them, and re-layouts  11.6 us (7%)
  other arithmetic  3.58 us (2%)
    ppermute x5, waiting for transfers between devices, from_behind(): return lax.ppermute(value, axis, pairs)  67 us
    all_gather x1, waiting for transfers between devices, body(): piece = lax.all_gather(tokens, 'tp', axis=0, tiled=True)  24.2 us
    ppermute x5, starting transfers between devices, from_behind(): return lax.ppermute(value, axis, pairs)  18.6 us
    all_to_all x1, starting transfers between devices, body(): lax.all_to_all(labels, 'seq', split_axis=0, concat_axis=0, tiled=True)  12.6 us
    all_to_all x1, starting transfers between devices, body(): lax.all_to_all(outgoing, 'seq', split_axis=0, concat_axis=0, tiled=True)  10.6 us
    pallas_call x1, Pallas kernels, attend(): pl.pallas_call(functools.partial(first_kernel, blocks=len(first), scale=s...  5.54 us
    pallas_call x1, Pallas kernels, attend(): pl.pallas_call(functools.partial(second_kernel, blocks=len(second), scale...  5.06 us
    unnamed x24, local copies, waits for them, and re-layouts  4.5 us
  transfers between devices with their start and end apart: 8, of which 5 were waited for; matrix products, arithmetic and copies ran while one was open for 6% of the time, Pallas kernels for 8%

profile of v6, /device:TPU:6, one launch (start us, length us, event | category | flops | bytes accessed | tf_op | source)
XLA Modules:
  0.0 177.2 jit_solution(18232405963662356652)
XLA Ops:
  7.2 0.0 all-gather.2.cloned.1.call-start
  7.2 0.7 all-gather.2.cloned.1.call-update
  7.9 0.2 convert_reduce_fusion.1
  8.1 0.1 select_reduce_fusion.1
  8.2 0.7 copy.35
  8.9 12.6 %all-to-all-start.1 = ((s32[64,1,1]{2,1,0:T(1,128)}), s32[64,1,1]{2,1,0:T(1,128)S(1)}, u32[]{:S(2)}, u32[]{:S(2)}) async-start(s32[64,1,1]{2,1,0:T(1,128)} %copy.35), calls=%async_computation.1 | async-start | bytes 65536 | tf_op jit(solution)/shard_map/all_to_all | solution.py:254
  21.6 0.0 copy-start.7
  21.6 0.6 copy-done.7
  22.2 0.1 copy.31
  22.4 0.1 multiply_reduce_fusion
  22.5 0.1 fusion.2
  22.6 0.5 fusion
  23.1 0.8 pad_maximum_fusion.1
  24.0 24.2 %all-gather.2.cloned.1.call-done.piece_ref = bf16[2048,256]{1,0:T(8,128)(2,1)} async-done(((bf16[256,256]{1,0:T(8,128)(2,1)}), bf16[2048,256]{1,0:T(8,128)(2,1)}) %all-gather.2.cloned.1.call-update) | async-done | bytes 1048592 | tf_op jit(solution)/shard_map/all_gather | solution.py:215
  48.2 3.4 %project_rotate.1.refs_0_.refs_5_ = bf16[256,512]{1,0:T(8,128)(2,1)} custom-call(bf16[2048,256]{1,0:T(8,128)(2,1)} %all-gather.2.cloned.1.call-done.piece_ref, bf16[2048,256]{1,0:T(8,128)(2,1)} %key_weight_ref.1, bf16[2048,256]{1,0:T(8,128)(2,1)} %value_weight_ref.1, f32[256,128]{1,0:T(8,128)} %get-tuple-element.27.cosine_ref, ...), custom_call_target="tpu_custom_call" | custom-call | flops 536870912 | bytes 3407872 | tf_op jit(solution)/shard_map/project_rotate/pallas_call | solution.py:72
  51.6 1.0 reshape.264
  52.6 1.6 gather_fusion
  54.2 0.0 all-to-all-done.1
  54.2 10.6 %all-to-all-start = ((bf16[64,16,2,256]{3,1,2,0:T(8,128)(2,1)}), bf16[64,16,2,256]{3,1,2,0:T(8,128)(2,1)S(1)}, u32[]{:S(2)}, u32[]{:S(2)}) async-start(bf16[64,16,2,256]{3,1,2,0:T(8,128)(2,1)} %gather_fusion), calls=%async_computation | async-start | bytes 2097152 | tf_op jit(solution)/shard_map/all_to_all | solution.py:253
  64.8 0.0 copy-done.6
  64.9 0.1 broadcast_add_fusion
  64.9 3.4 %collective-permute-start = (bf16[256,512]{1,0:T(8,128)(2,1)S(1)}, bf16[256,512]{1,0:T(8,128)(2,1)S(1)}, u32[]{:S(2)}, u32[]{:S(2)}) collective-permute-start(bf16[256,512]{1,0:T(8,128)(2,1)S(1)} %copy-done.1), channel_id=1, source_target_pairs={{0,8},{8,16},{16,24},{24,32},{32,40},{40,48},{48,56},{56,64},{64,7... | collective-permute-start | bytes 786440 | tf_op jit(solution)/shard_map/ppermute | solution.py:21
  68.3 6.4 %collective-permute-start.1 = (bf16[256,512]{1,0:T(8,128)(2,1)S(1)}, bf16[256,512]{1,0:T(8,128)(2,1)S(1)}, u32[]{:S(2)}, u32[]{:S(2)}) collective-permute-start(bf16[256,512]{1,0:T(8,128)(2,1)S(1)} %copy-done.1), channel_id=1, source_target_pairs={{0,24},{8,32},{16,40},{24,48},{32,56},{40,64},{48,72},{56,80},{64,... | collective-permute-start | bytes 786440 | tf_op jit(solution)/shard_map/ppermute | solution.py:21
  74.7 0.1 convert_reduce_fusion
  74.8 0.8 copy.33.query_segment_ref
  75.6 0.1 compare_select_fusion.1
  75.7 0.6 slice.12.key_segment_ref
  76.3 0.7 copy.37
  77.0 1.2 reduce.3
  78.2 21.6 %collective-permute-done.refs_1_.refs_6_ = bf16[256,512]{1,0:T(8,128)(2,1)S(1)} collective-permute-done((bf16[256,512]{1,0:T(8,128)(2,1)S(1)}, bf16[256,512]{1,0:T(8,128)(2,1)S(1)}, u32[]{:S(2)}, u32[]{:S(2)}) %collective-permute-start) | collective-permute-done | bytes 262176 | tf_op jit(solution)/shard_map/ppermute | solution.py:21
  99.8 14.7 %collective-permute-done.1.refs_2_.refs_7_ = bf16[256,512]{1,0:T(8,128)(2,1)S(1)} collective-permute-done((bf16[256,512]{1,0:T(8,128)(2,1)S(1)}, bf16[256,512]{1,0:T(8,128)(2,1)S(1)}, u32[]{:S(2)}, u32[]{:S(2)}) %collective-permute-start.1) | collective-permute-done | bytes 262176 | tf_op jit(solution)/shard_map/ppermute | solution.py:21
  114.5 0.1 pad_maximum_fusion
  114.6 0.6 copy-done.4
  115.2 2.7 %collective-permute-start.4 = (bf16[256,1024]{1,0:T(8,128)(2,1)S(1)}, bf16[256,1024]{1,0:T(8,128)(2,1)S(1)}, u32[]{:S(2)}, u32[]{:S(2)}) collective-permute-start(bf16[256,1024]{1,0:T(8,128)(2,1)S(1)} %pad_maximum_fusion), channel_id=1, source_target_pairs={{0,8},{8,16},{16,24},{24,32},{32,40},{40,48},{48,56},{56,64},{64,7... | collective-permute-start | bytes 1572872 | tf_op jit(solution)/shard_map/ppermute | solution.py:21
  117.9 0.1 select_reduce_fusion
  118.0 3.0 %collective-permute-start.2 = (bf16[256,512]{1,0:T(8,128)(2,1)S(1)}, bf16[256,512]{1,0:T(8,128)(2,1)S(1)}, u32[]{:S(2)}, u32[]{:S(2)}) collective-permute-start(bf16[256,512]{1,0:T(8,128)(2,1)S(1)} %copy-done.1), channel_id=1, source_target_pairs={{0,40},{8,48},{16,56},{24,64},{32,72},{40,80},{48,88},{56,96},{64,... | collective-permute-start | bytes 786440 | tf_op jit(solution)/shard_map/ppermute | solution.py:21
  121.0 3.1 %collective-permute-start.3 = (bf16[256,512]{1,0:T(8,128)(2,1)S(1)}, bf16[256,512]{1,0:T(8,128)(2,1)S(1)}, u32[]{:S(2)}, u32[]{:S(2)}) collective-permute-start(bf16[256,512]{1,0:T(8,128)(2,1)S(1)} %copy-done.1), channel_id=1, source_target_pairs={{0,48},{8,56},{16,64},{24,72},{32,80},{40,88},{48,96},{56,104},{64... | collective-permute-start | bytes 786440 | tf_op jit(solution)/shard_map/ppermute | solution.py:21
  124.2 17.5 %collective-permute-done.2.refs_3_.refs_8_ = bf16[256,512]{1,0:T(8,128)(2,1)S(1)} collective-permute-done((bf16[256,512]{1,0:T(8,128)(2,1)S(1)}, bf16[256,512]{1,0:T(8,128)(2,1)S(1)}, u32[]{:S(2)}, u32[]{:S(2)}) %collective-permute-start.2) | collective-permute-done | bytes 262176 | tf_op jit(solution)/shard_map/ppermute | solution.py:21
  141.6 13.3 %collective-permute-done.3.refs_4_.refs_9_ = bf16[256,512]{1,0:T(8,128)(2,1)S(1)} collective-permute-done((bf16[256,512]{1,0:T(8,128)(2,1)S(1)}, bf16[256,512]{1,0:T(8,128)(2,1)S(1)}, u32[]{:S(2)}, u32[]{:S(2)}) %collective-permute-start.3) | collective-permute-done | bytes 262176 | tf_op jit(solution)/shard_map/ppermute | solution.py:21
  155.0 0.7 copy-done.9
  155.7 5.5 %first_blocks.1 = (f32[256,512]{1,0:T(8,128)}, f32[256,512]{1,0:T(8,128)}, f32[256,512]{1,0:T(8,128)}) custom-call(s32[256,1]{1,0:T(8,128)} %copy.33.query_segment_ref, s32[5,256]{1,0:T(8,128)} %bitcast.18, bf16[256,512]{1,0:T(8,128)(2,1)} %bitcast.15, bf16[256,512]{1,0:T(8,128)(2,1)} %project_rotate.1.refs_0_.refs_5_, bf16[256,512]{1,0:T(8,128)(2,1)} %copy-done.3, ...), custom_call_target="tpu_custom_call" | custom-call | flops 1006632960 | bytes 3145728 | tf_op jit(solution)/shard_map/first_blocks/pallas_call | solution.py:186
  161.2 0.0 collective-permute-done.4.refs_0_.refs_1_.refs_2_.refs_3_
  161.2 0.8 copy-done
  162.0 5.1 %second_blocks.1 = bf16[256,512]{1,0:T(8,128)(2,1)} custom-call(s32[256,1]{1,0:T(8,128)} %copy.33.query_segment_ref, s32[2,256]{1,0:T(2,128)} %slice.12.key_segment_ref, bf16[256,512]{1,0:T(8,128)(2,1)} %bitcast.16, f32[256,512]{1,0:T(8,128)} %get-tuple-element.5.peak_ref, f32[256,512]{1,0:T(8,128)} %get-tuple-element.6.total_ref, ...), custom_call_target="tpu_custom_call" | custom-call | flops 402653184 | bytes 2359296 | tf_op jit(solution)/shard_map/second_blocks/pallas_call | solution.py:196
  167.1 1.7 reshape.263
  168.8 0.0 all-to-all-done
  168.8 0.6 gather_fusion.1
  169.4 0.9 copy.36
  (30 shorter events, 0.2 us)
Async XLA Ops:
  7.2 0.7 copy-start.10
  7.2 41.0 %all-gather.2.cloned.1.call-start = ((), (), s32[]{:S(2)}) async-start(), calls=%async_computation.2 | async-start | bytes 1179648 | tf_op jit(solution)/shard_map/all_gather | solution.py:215
  8.9 45.3 %all-to-all-start.1 = ((s32[64,1,1]{2,1,0:T(1,128)}), s32[64,1,1]{2,1,0:T(1,128)S(1)}, u32[]{:S(2)}, u32[]{:S(2)}) async-start(s32[64,1,1]{2,1,0:T(1,128)} %copy.35), calls=%async_computation.1 | async-start | bytes 65536 | tf_op jit(solution)/shard_map/all_to_all | solution.py:254
  21.6 0.7 copy-start.7
  54.2 10.6 %copy-start.6 = (s32[7]{0:T(128)S(1)}, s32[7]{0:T(128)}, u32[]{:S(2)}) copy-start(s32[7]{0:T(128)} %constant.68) | copy-start | bytes 88
  54.2 10.7 %copy-start.1 = (bf16[256,512]{1,0:T(8,128)(2,1)S(1)}, bf16[256,512]{1,0:T(8,128)(2,1)}, u32[]{:S(2)}) copy-start(bf16[256,512]{1,0:T(8,128)(2,1)} %project_rotate.1.refs_0_.refs_5_) | copy-start | bytes 786436
  54.2 22.0 %copy-start.2 = (bf16[256,2,256]{2,1,0:T(2,128)(2,1)S(1)}, bf16[256,2,256]{2,1,0:T(2,128)(2,1)}, u32[]{:S(2)}) copy-start(bf16[256,2,256]{2,1,0:T(2,128)(2,1)} %param.10) | copy-start | bytes 786436
  54.2 114.6 %all-to-all-start = ((bf16[64,16,2,256]{3,1,2,0:T(8,128)(2,1)}), bf16[64,16,2,256]{3,1,2,0:T(8,128)(2,1)S(1)}, u32[]{:S(2)}, u32[]{:S(2)}) async-start(bf16[64,16,2,256]{3,1,2,0:T(8,128)(2,1)} %gather_fusion), calls=%async_computation | async-start | bytes 2097152 | tf_op jit(solution)/shard_map/all_to_all | solution.py:253
  64.9 34.9 %collective-permute-start = (bf16[256,512]{1,0:T(8,128)(2,1)S(1)}, bf16[256,512]{1,0:T(8,128)(2,1)S(1)}, u32[]{:S(2)}, u32[]{:S(2)}) collective-permute-start(bf16[256,512]{1,0:T(8,128)(2,1)S(1)} %copy-done.1), channel_id=1, source_target_pairs={{0,8},{8,16},{16,24},{24,32},{32,40},{40,48},{48,56},{56,64},{64,7... | collective-permute-start | bytes 786440 | tf_op jit(solution)/shard_map/ppermute | solution.py:21
  68.3 46.2 %collective-permute-start.1 = (bf16[256,512]{1,0:T(8,128)(2,1)S(1)}, bf16[256,512]{1,0:T(8,128)(2,1)S(1)}, u32[]{:S(2)}, u32[]{:S(2)}) collective-permute-start(bf16[256,512]{1,0:T(8,128)(2,1)S(1)} %copy-done.1), channel_id=1, source_target_pairs={{0,24},{8,32},{16,40},{24,48},{32,56},{40,64},{48,72},{56,80},{64,... | collective-permute-start | bytes 786440 | tf_op jit(solution)/shard_map/ppermute | solution.py:21
  75.7 1.3 copy-start.5
  99.8 14.7 %copy-start.3 = (bf16[256,512]{1,0:T(8,128)(2,1)}, bf16[256,512]{1,0:T(8,128)(2,1)S(1)}, u32[]{:S(2)}) copy-start(bf16[256,512]{1,0:T(8,128)(2,1)S(1)} %collective-permute-done.refs_1_.refs_6_) | copy-start | bytes 786436
  114.5 0.7 copy-start.4
  115.2 46.0 %collective-permute-start.4 = (bf16[256,1024]{1,0:T(8,128)(2,1)S(1)}, bf16[256,1024]{1,0:T(8,128)(2,1)S(1)}, u32[]{:S(2)}, u32[]{:S(2)}) collective-permute-start(bf16[256,1024]{1,0:T(8,128)(2,1)S(1)} %pad_maximum_fusion), channel_id=1, source_target_pairs={{0,8},{8,16},{16,24},{24,32},{32,40},{40,48},{48,56},{56,64},{64,7... | collective-permute-start | bytes 1572872 | tf_op jit(solution)/shard_map/ppermute | solution.py:21
  118.0 23.6 %collective-permute-start.2 = (bf16[256,512]{1,0:T(8,128)(2,1)S(1)}, bf16[256,512]{1,0:T(8,128)(2,1)S(1)}, u32[]{:S(2)}, u32[]{:S(2)}) collective-permute-start(bf16[256,512]{1,0:T(8,128)(2,1)S(1)} %copy-done.1), channel_id=1, source_target_pairs={{0,40},{8,48},{16,56},{24,64},{32,72},{40,80},{48,88},{56,96},{64,... | collective-permute-start | bytes 786440 | tf_op jit(solution)/shard_map/ppermute | solution.py:21
  121.0 33.9 %collective-permute-start.3 = (bf16[256,512]{1,0:T(8,128)(2,1)S(1)}, bf16[256,512]{1,0:T(8,128)(2,1)S(1)}, u32[]{:S(2)}, u32[]{:S(2)}) collective-permute-start(bf16[256,512]{1,0:T(8,128)(2,1)S(1)} %copy-done.1), channel_id=1, source_target_pairs={{0,48},{8,56},{16,64},{24,72},{32,80},{40,88},{48,96},{56,104},{64... | collective-permute-start | bytes 786440 | tf_op jit(solution)/shard_map/ppermute | solution.py:21
  141.6 13.3 %copy-start.8 = (bf16[256,512]{1,0:T(8,128)(2,1)}, bf16[256,512]{1,0:T(8,128)(2,1)S(1)}, u32[]{:S(2)}) copy-start(bf16[256,512]{1,0:T(8,128)(2,1)S(1)} %collective-permute-done.2.refs_3_.refs_8_) | copy-start | bytes 786436
  155.0 0.7 copy-start.9
  161.2 0.8 copy-start
Sparse Core Ops, SparseCore 0:
  10.1 38.0 all-gather.1

commit v7 on v5

--- a/solution.py
+++ b/solution.py
@@ -229,7 +229,8 @@
     key_segment = jnp.where(key_place >= 0, key_segment.reshape(len(order), block_rows), -1)
     key_segment = (key_segment[: len(first)], key_segment[len(first) :])
     query = queries.reshape(block_rows, TOPK * width)
-    attended = attend(query, segment[:, None], key_segment, first, second, local_heads)
+    query_segment = segment[:, None]
+    attended = attend(query, query_segment, key_segment, first, second, local_heads)
     attended = attended.reshape(block_rows, TOPK, width)
     pages_dev = block_rows // PAGE
     capacity = max(1, pages_dev // devices)
@@ -248,8 +249,9 @@
     incoming = lax.all_to_all(outgoing, "seq", split_axis=0, concat_axis=0, tiled=True)
     arrived = lax.all_to_all(labels, "seq", split_axis=0, concat_axis=0, tiled=True)
     slots = jnp.arange(devices * capacity, dtype=jnp.int32)
+    arrived = arrived.reshape(devices * capacity, 1)
     source_slot = jnp.sum(
-        jnp.where(arrived.reshape(-1)[None, :] == page_order[:, None], slots[None, :], 0), axis=1
+        jnp.where(arrived == page_order[None, :], slots[:, None], 0), axis=0
     )
     cache = incoming[source_slot]
     return (attended, cache)

time: 178 us -> 178 us (level)
  no operation moved by 1% of the time
where the time goes in v7:
time: 178 us; the launch traced here: 177 us
  waiting for transfers between devices  92 us (52%)
  starting transfers between devices  41.8 us (23%)
  between operations  14.3 us (8%)
  Pallas kernels  14 us (8%)
  local copies, waits for them, and re-layouts  11.6 us (7%)
  other arithmetic  3.58 us (2%)
    ppermute x5, waiting for transfers between devices, from_behind(): return lax.ppermute(value, axis, pairs)  67 us
    all_gather x1, waiting for transfers between devices, body(): piece = lax.all_gather(tokens, 'tp', axis=0, tiled=True)  24.2 us
    ppermute x5, starting transfers between devices, from_behind(): return lax.ppermute(value, axis, pairs)  18.6 us
    all_to_all x1, starting transfers between devices, body(): lax.all_to_all(labels, 'seq', split_axis=0, concat_axis=0, tiled=True)  12.6 us
    all_to_all x1, starting transfers between devices, body(): lax.all_to_all(outgoing, 'seq', split_axis=0, concat_axis=0, tiled=True)  10.6 us
    pallas_call x1, Pallas kernels, attend(): pl.pallas_call(functools.partial(first_kernel, blocks=len(first), scale=s...  5.54 us
    pallas_call x1, Pallas kernels, attend(): pl.pallas_call(functools.partial(second_kernel, blocks=len(second), scale...  5.06 us
    unnamed x24, local copies, waits for them, and re-layouts  4.5 us
  transfers between devices with their start and end apart: 8, of which 5 were waited for; matrix products, arithmetic and copies ran while one was open for 6% of the time, Pallas kernels for 8%

profile of v7, /device:TPU:6, one launch (start us, length us, event | category | flops | bytes accessed | tf_op | source)
XLA Modules:
  0.0 177.2 jit_solution(18232405963662356652)
XLA Ops:
  7.2 0.0 all-gather.2.cloned.1.call-start
  7.2 0.7 all-gather.2.cloned.1.call-update
  7.9 0.2 convert_reduce_fusion.1
  8.1 0.1 select_reduce_fusion.1
  8.2 0.7 copy.35
  8.9 12.6 %all-to-all-start.1 = ((s32[64,1,1]{2,1,0:T(1,128)}), s32[64,1,1]{2,1,0:T(1,128)S(1)}, u32[]{:S(2)}, u32[]{:S(2)}) async-start(s32[64,1,1]{2,1,0:T(1,128)} %copy.35), calls=%async_computation.1 | async-start | bytes 65536 | tf_op jit(solution)/shard_map/all_to_all | solution.py:250
  21.6 0.0 copy-start.7
  21.6 0.6 copy-done.7
  22.2 0.1 copy.31
  22.4 0.1 multiply_reduce_fusion
  22.5 0.1 fusion.2
  22.6 0.5 fusion
  23.1 0.8 pad_maximum_fusion.1
  24.0 24.2 %all-gather.2.cloned.1.call-done.piece_ref = bf16[2048,256]{1,0:T(8,128)(2,1)} async-done(((bf16[256,256]{1,0:T(8,128)(2,1)}), bf16[2048,256]{1,0:T(8,128)(2,1)}) %all-gather.2.cloned.1.call-update) | async-done | bytes 1048592 | tf_op jit(solution)/shard_map/all_gather | solution.py:215
  48.2 3.4 %project_rotate.1.refs_0_.refs_5_ = bf16[256,512]{1,0:T(8,128)(2,1)} custom-call(bf16[2048,256]{1,0:T(8,128)(2,1)} %all-gather.2.cloned.1.call-done.piece_ref, bf16[2048,256]{1,0:T(8,128)(2,1)} %key_weight_ref.1, bf16[2048,256]{1,0:T(8,128)(2,1)} %value_weight_ref.1, f32[256,128]{1,0:T(8,128)} %get-tuple-element.27.cosine_ref, ...), custom_call_target="tpu_custom_call" | custom-call | flops 536870912 | bytes 3407872 | tf_op jit(solution)/shard_map/project_rotate/pallas_call | solution.py:72
  51.6 1.0 reshape.263
  52.6 1.6 gather_fusion
  54.2 0.0 all-to-all-done.1
  54.2 10.6 %all-to-all-start = ((bf16[64,16,2,256]{3,1,2,0:T(8,128)(2,1)}), bf16[64,16,2,256]{3,1,2,0:T(8,128)(2,1)S(1)}, u32[]{:S(2)}, u32[]{:S(2)}) async-start(bf16[64,16,2,256]{3,1,2,0:T(8,128)(2,1)} %gather_fusion), calls=%async_computation | async-start | bytes 2097152 | tf_op jit(solution)/shard_map/all_to_all | solution.py:249
  64.8 0.0 copy-done.6
  64.9 0.1 broadcast_add_fusion
  64.9 3.4 %collective-permute-start = (bf16[256,512]{1,0:T(8,128)(2,1)S(1)}, bf16[256,512]{1,0:T(8,128)(2,1)S(1)}, u32[]{:S(2)}, u32[]{:S(2)}) collective-permute-start(bf16[256,512]{1,0:T(8,128)(2,1)S(1)} %copy-done.1), channel_id=1, source_target_pairs={{0,8},{8,16},{16,24},{24,32},{32,40},{40,48},{48,56},{56,64},{64,7... | collective-permute-start | bytes 786440 | tf_op jit(solution)/shard_map/ppermute | solution.py:21
  68.3 6.4 %collective-permute-start.1 = (bf16[256,512]{1,0:T(8,128)(2,1)S(1)}, bf16[256,512]{1,0:T(8,128)(2,1)S(1)}, u32[]{:S(2)}, u32[]{:S(2)}) collective-permute-start(bf16[256,512]{1,0:T(8,128)(2,1)S(1)} %copy-done.1), channel_id=1, source_target_pairs={{0,24},{8,32},{16,40},{24,48},{32,56},{40,64},{48,72},{56,80},{64,... | collective-permute-start | bytes 786440 | tf_op jit(solution)/shard_map/ppermute | solution.py:21
  74.7 0.1 convert_reduce_fusion
  74.8 0.8 copy.33.query_segment_ref
  75.6 0.1 compare_select_fusion.1
  75.7 0.6 slice.12.key_segment_ref
  76.3 0.7 copy.37
  77.0 1.2 reduce.3
  78.2 21.6 %collective-permute-done.refs_1_.refs_6_ = bf16[256,512]{1,0:T(8,128)(2,1)S(1)} collective-permute-done((bf16[256,512]{1,0:T(8,128)(2,1)S(1)}, bf16[256,512]{1,0:T(8,128)(2,1)S(1)}, u32[]{:S(2)}, u32[]{:S(2)}) %collective-permute-start) | collective-permute-done | bytes 262176 | tf_op jit(solution)/shard_map/ppermute | solution.py:21
  99.8 14.7 %collective-permute-done.1.refs_2_.refs_7_ = bf16[256,512]{1,0:T(8,128)(2,1)S(1)} collective-permute-done((bf16[256,512]{1,0:T(8,128)(2,1)S(1)}, bf16[256,512]{1,0:T(8,128)(2,1)S(1)}, u32[]{:S(2)}, u32[]{:S(2)}) %collective-permute-start.1) | collective-permute-done | bytes 262176 | tf_op jit(solution)/shard_map/ppermute | solution.py:21
  114.5 0.1 pad_maximum_fusion
  114.6 0.6 copy-done.4
  115.2 2.7 %collective-permute-start.4 = (bf16[256,1024]{1,0:T(8,128)(2,1)S(1)}, bf16[256,1024]{1,0:T(8,128)(2,1)S(1)}, u32[]{:S(2)}, u32[]{:S(2)}) collective-permute-start(bf16[256,1024]{1,0:T(8,128)(2,1)S(1)} %pad_maximum_fusion), channel_id=1, source_target_pairs={{0,8},{8,16},{16,24},{24,32},{32,40},{40,48},{48,56},{56,64},{64,7... | collective-permute-start | bytes 1572872 | tf_op jit(solution)/shard_map/ppermute | solution.py:21
  117.9 0.1 select_reduce_fusion
  118.0 3.0 %collective-permute-start.2 = (bf16[256,512]{1,0:T(8,128)(2,1)S(1)}, bf16[256,512]{1,0:T(8,128)(2,1)S(1)}, u32[]{:S(2)}, u32[]{:S(2)}) collective-permute-start(bf16[256,512]{1,0:T(8,128)(2,1)S(1)} %copy-done.1), channel_id=1, source_target_pairs={{0,40},{8,48},{16,56},{24,64},{32,72},{40,80},{48,88},{56,96},{64,... | collective-permute-start | bytes 786440 | tf_op jit(solution)/shard_map/ppermute | solution.py:21
  121.0 3.1 %collective-permute-start.3 = (bf16[256,512]{1,0:T(8,128)(2,1)S(1)}, bf16[256,512]{1,0:T(8,128)(2,1)S(1)}, u32[]{:S(2)}, u32[]{:S(2)}) collective-permute-start(bf16[256,512]{1,0:T(8,128)(2,1)S(1)} %copy-done.1), channel_id=1, source_target_pairs={{0,48},{8,56},{16,64},{24,72},{32,80},{40,88},{48,96},{56,104},{64... | collective-permute-start | bytes 786440 | tf_op jit(solution)/shard_map/ppermute | solution.py:21
  124.2 17.5 %collective-permute-done.2.refs_3_.refs_8_ = bf16[256,512]{1,0:T(8,128)(2,1)S(1)} collective-permute-done((bf16[256,512]{1,0:T(8,128)(2,1)S(1)}, bf16[256,512]{1,0:T(8,128)(2,1)S(1)}, u32[]{:S(2)}, u32[]{:S(2)}) %collective-permute-start.2) | collective-permute-done | bytes 262176 | tf_op jit(solution)/shard_map/ppermute | solution.py:21
  141.6 13.3 %collective-permute-done.3.refs_4_.refs_9_ = bf16[256,512]{1,0:T(8,128)(2,1)S(1)} collective-permute-done((bf16[256,512]{1,0:T(8,128)(2,1)S(1)}, bf16[256,512]{1,0:T(8,128)(2,1)S(1)}, u32[]{:S(2)}, u32[]{:S(2)}) %collective-permute-start.3) | collective-permute-done | bytes 262176 | tf_op jit(solution)/shard_map/ppermute | solution.py:21
  155.0 0.7 copy-done.9
  155.7 5.5 %first_blocks.1 = (f32[256,512]{1,0:T(8,128)}, f32[256,512]{1,0:T(8,128)}, f32[256,512]{1,0:T(8,128)}) custom-call(s32[256,1]{1,0:T(8,128)} %copy.33.query_segment_ref, s32[5,256]{1,0:T(8,128)} %bitcast.18, bf16[256,512]{1,0:T(8,128)(2,1)} %bitcast.15, bf16[256,512]{1,0:T(8,128)(2,1)} %project_rotate.1.refs_0_.refs_5_, bf16[256,512]{1,0:T(8,128)(2,1)} %copy-done.3, ...), custom_call_target="tpu_custom_call" | custom-call | flops 1006632960 | bytes 3145728 | tf_op jit(solution)/shard_map/first_blocks/pallas_call | solution.py:186
  161.2 0.0 collective-permute-done.4.refs_0_.refs_1_.refs_2_.refs_3_
  161.2 0.8 copy-done
  162.0 5.1 %second_blocks.1 = bf16[256,512]{1,0:T(8,128)(2,1)} custom-call(s32[256,1]{1,0:T(8,128)} %copy.33.query_segment_ref, s32[2,256]{1,0:T(2,128)} %slice.12.key_segment_ref, bf16[256,512]{1,0:T(8,128)(2,1)} %bitcast.16, f32[256,512]{1,0:T(8,128)} %get-tuple-element.5.peak_ref, f32[256,512]{1,0:T(8,128)} %get-tuple-element.6.total_ref, ...), custom_call_target="tpu_custom_call" | custom-call | flops 402653184 | bytes 2359296 | tf_op jit(solution)/shard_map/second_blocks/pallas_call | solution.py:196
  167.1 1.7 reshape.262
  168.8 0.0 all-to-all-done
  168.8 0.6 gather_fusion.1
  169.4 0.9 copy.36
  (30 shorter events, 0.2 us)
Async XLA Ops:
  7.2 0.7 copy-start.10
  7.2 41.0 %all-gather.2.cloned.1.call-start = ((), (), s32[]{:S(2)}) async-start(), calls=%async_computation.2 | async-start | bytes 1179648 | tf_op jit(solution)/shard_map/all_gather | solution.py:215
  8.9 45.3 %all-to-all-start.1 = ((s32[64,1,1]{2,1,0:T(1,128)}), s32[64,1,1]{2,1,0:T(1,128)S(1)}, u32[]{:S(2)}, u32[]{:S(2)}) async-start(s32[64,1,1]{2,1,0:T(1,128)} %copy.35), calls=%async_computation.1 | async-start | bytes 65536 | tf_op jit(solution)/shard_map/all_to_all | solution.py:250
  21.6 0.7 copy-start.7
  54.2 10.6 %copy-start.6 = (s32[7]{0:T(128)S(1)}, s32[7]{0:T(128)}, u32[]{:S(2)}) copy-start(s32[7]{0:T(128)} %constant.68) | copy-start | bytes 88
  54.2 10.7 %copy-start.1 = (bf16[256,512]{1,0:T(8,128)(2,1)S(1)}, bf16[256,512]{1,0:T(8,128)(2,1)}, u32[]{:S(2)}) copy-start(bf16[256,512]{1,0:T(8,128)(2,1)} %project_rotate.1.refs_0_.refs_5_) | copy-start | bytes 786436
  54.2 22.0 %copy-start.2 = (bf16[256,2,256]{2,1,0:T(2,128)(2,1)S(1)}, bf16[256,2,256]{2,1,0:T(2,128)(2,1)}, u32[]{:S(2)}) copy-start(bf16[256,2,256]{2,1,0:T(2,128)(2,1)} %param.10) | copy-start | bytes 786436
  54.2 114.6 %all-to-all-start = ((bf16[64,16,2,256]{3,1,2,0:T(8,128)(2,1)}), bf16[64,16,2,256]{3,1,2,0:T(8,128)(2,1)S(1)}, u32[]{:S(2)}, u32[]{:S(2)}) async-start(bf16[64,16,2,256]{3,1,2,0:T(8,128)(2,1)} %gather_fusion), calls=%async_computation | async-start | bytes 2097152 | tf_op jit(solution)/shard_map/all_to_all | solution.py:249
  64.9 34.9 %collective-permute-start = (bf16[256,512]{1,0:T(8,128)(2,1)S(1)}, bf16[256,512]{1,0:T(8,128)(2,1)S(1)}, u32[]{:S(2)}, u32[]{:S(2)}) collective-permute-start(bf16[256,512]{1,0:T(8,128)(2,1)S(1)} %copy-done.1), channel_id=1, source_target_pairs={{0,8},{8,16},{16,24},{24,32},{32,40},{40,48},{48,56},{56,64},{64,7... | collective-permute-start | bytes 786440 | tf_op jit(solution)/shard_map/ppermute | solution.py:21
  68.3 46.2 %collective-permute-start.1 = (bf16[256,512]{1,0:T(8,128)(2,1)S(1)}, bf16[256,512]{1,0:T(8,128)(2,1)S(1)}, u32[]{:S(2)}, u32[]{:S(2)}) collective-permute-start(bf16[256,512]{1,0:T(8,128)(2,1)S(1)} %copy-done.1), channel_id=1, source_target_pairs={{0,24},{8,32},{16,40},{24,48},{32,56},{40,64},{48,72},{56,80},{64,... | collective-permute-start | bytes 786440 | tf_op jit(solution)/shard_map/ppermute | solution.py:21
  75.7 1.3 copy-start.5
  99.8 14.7 %copy-start.3 = (bf16[256,512]{1,0:T(8,128)(2,1)}, bf16[256,512]{1,0:T(8,128)(2,1)S(1)}, u32[]{:S(2)}) copy-start(bf16[256,512]{1,0:T(8,128)(2,1)S(1)} %collective-permute-done.refs_1_.refs_6_) | copy-start | bytes 786436
  114.5 0.7 copy-start.4
  115.2 46.0 %collective-permute-start.4 = (bf16[256,1024]{1,0:T(8,128)(2,1)S(1)}, bf16[256,1024]{1,0:T(8,128)(2,1)S(1)}, u32[]{:S(2)}, u32[]{:S(2)}) collective-permute-start(bf16[256,1024]{1,0:T(8,128)(2,1)S(1)} %pad_maximum_fusion), channel_id=1, source_target_pairs={{0,8},{8,16},{16,24},{24,32},{32,40},{40,48},{48,56},{56,64},{64,7... | collective-permute-start | bytes 1572872 | tf_op jit(solution)/shard_map/ppermute | solution.py:21
  118.0 23.6 %collective-permute-start.2 = (bf16[256,512]{1,0:T(8,128)(2,1)S(1)}, bf16[256,512]{1,0:T(8,128)(2,1)S(1)}, u32[]{:S(2)}, u32[]{:S(2)}) collective-permute-start(bf16[256,512]{1,0:T(8,128)(2,1)S(1)} %copy-done.1), channel_id=1, source_target_pairs={{0,40},{8,48},{16,56},{24,64},{32,72},{40,80},{48,88},{56,96},{64,... | collective-permute-start | bytes 786440 | tf_op jit(solution)/shard_map/ppermute | solution.py:21
  121.0 33.9 %collective-permute-start.3 = (bf16[256,512]{1,0:T(8,128)(2,1)S(1)}, bf16[256,512]{1,0:T(8,128)(2,1)S(1)}, u32[]{:S(2)}, u32[]{:S(2)}) collective-permute-start(bf16[256,512]{1,0:T(8,128)(2,1)S(1)} %copy-done.1), channel_id=1, source_target_pairs={{0,48},{8,56},{16,64},{24,72},{32,80},{40,88},{48,96},{56,104},{64... | collective-permute-start | bytes 786440 | tf_op jit(solution)/shard_map/ppermute | solution.py:21
  141.6 13.3 %copy-start.8 = (bf16[256,512]{1,0:T(8,128)(2,1)}, bf16[256,512]{1,0:T(8,128)(2,1)S(1)}, u32[]{:S(2)}) copy-start(bf16[256,512]{1,0:T(8,128)(2,1)S(1)} %collective-permute-done.2.refs_3_.refs_8_) | copy-start | bytes 786436
  155.0 0.7 copy-start.9
  161.2 0.8 copy-start
Sparse Core Ops, SparseCore 0:
  10.1 38.0 all-gather.1
